TPU v7x, 256 devices: a whole 4x4x8 slice. The times are simulated.
256 devices in a mesh: cfg: 2 (over x_hi), gx: 8 (over y, x_lo), gy: 16 (over z, core).
Axes of the slice: x: 4 (x_hi: 2, x_lo: 2; x = x_hi * 2 + x_lo), y: 4, z: 8, core: 2. Of those that a mesh axis runs over, the one named last changes fastest.
Arguments:
- descriptors: bfloat16 [2, 8, 32, 64, 128], P('cfg', 'gx', 'gy'), may hold values from -0.5 to 0.5
- derivatives: bfloat16 [2, 8, 32, 64, 16, 3, 128], P('cfg', 'gx', 'gy'), may hold values from -6 to 6
- neighbours: int32 [2, 8, 32, 64, 16], P('cfg', 'gx', 'gy'), may hold values from 0 to 575
- valid: int32 [2, 8, 32, 64], P('cfg', 'gx', 'gy'), may hold values from 0 to 1, as said below
- forces: bfloat16 [2, 8, 32, 64, 3], P('cfg', 'gx', 'gy'), may hold values from -6 to 6
- pool: bfloat16 [2048, 128], replicated, may hold values from -0.5 to 0.5
- sparse_idx: int32 [1024], replicated, may hold values from 0 to 2047, as said below
Outputs:
- design: bfloat16 [2, 8, 32, 64, 3, 1024], P('cfg', 'gx', 'gy')
- gram: float32 [1024, 1024], P(('gx', 'gy'))
- rhs: float32 [1024], P(('gx', 'gy'))
Inputs may be any that keep to these rules, and one draw needn't show every extreme that they name: `valid`: the first atom of every tile is real. `sparse_idx`: distinct rows.
All inputs are finite; a program needn't handle non-finite values.
Results may differ from a plain program's by a relative error of at most 0.0031.
Values sent between devices are 32-bit elements; how exact they have to be, the bound alone decides.
No kernel may reach another device: no remote copies, remote signals or barrier semaphores. Data moves between devices by JAX's collectives and lax.ppermute only.
A program may use at most 128 MiB of HBM per device.

v0:
```python
import jax
import jax.numpy as jnp
from jax import lax
from jax.sharding import PartitionSpec as P


def passed_along(x, axis, by):
    length = lax.axis_size(axis)
    return lax.ppermute(x, axis, [(i, (i + by) % length) for i in range(length)])


def project_rows(left, sparse):
    return lax.dot_general(
        left, sparse, (((1,), (1,)), ((), ())), preferred_element_type=jnp.float32
    )


def fold_x(slab_array):
    inner_count = slab_array.shape[0] - 2
    from_high = passed_along(slab_array[0], "gx", -1)
    from_low = passed_along(slab_array[inner_count + 1], "gx", 1)
    interior = slab_array[1 : inner_count + 1]
    interior = interior.at[inner_count - 1].add(from_high)
    interior = interior.at[0].add(from_low)
    return interior


def fold_y(slab_array):
    inner_count = slab_array.shape[1] - 2
    from_high = passed_along(slab_array[:, 0], "gy", -1)
    from_low = passed_along(slab_array[:, inner_count + 1], "gy", 1)
    interior = slab_array[:, 1 : inner_count + 1]
    interior = interior.at[:, inner_count - 1].add(from_high)
    interior = interior.at[:, 0].add(from_low)
    return interior


def per_device(descriptors, derivatives, neighbours, valid, forces, pool, sparse_idx):
    tiles_x = descriptors.shape[1]
    tiles_y = descriptors.shape[2]
    slot_total = derivatives.shape[4]
    desc_width = descriptors.shape[4]
    sparse = pool[sparse_idx]
    sparse_count = sparse.shape[0]
    flat_desc = descriptors.reshape(tiles_x * tiles_y, 64, desc_width)
    flat_deriv = derivatives.reshape(tiles_x * tiles_y, 64 * slot_total * 3, desc_width)
    flat_nbr = neighbours.reshape(tiles_x * tiles_y, 64, slot_total)
    flat_valid = valid.reshape(tiles_x * tiles_y, 64)
    accumulator = jnp.zeros(((tiles_x + 2) * (tiles_y + 2) * 64, 3, sparse_count), jnp.float32)

    def add_tile(tile_step, accumulator):
        tile_x = tile_step // tiles_y
        tile_y = tile_step % tiles_y
        desc_tile = lax.dynamic_index_in_dim(flat_desc, tile_step, 0, keepdims=False)
        deriv_tile = lax.dynamic_index_in_dim(flat_deriv, tile_step, 0, keepdims=False)
        nbr_tile = lax.dynamic_index_in_dim(flat_nbr, tile_step, 0, keepdims=False)
        valid_tile = lax.dynamic_index_in_dim(flat_valid, tile_step, 0, keepdims=False)
        scores = project_rows(desc_tile, sparse) * valid_tile[:, None].astype(jnp.float32)
        projected = project_rows(deriv_tile, sparse).reshape(64, slot_total, 3, sparse_count)
        contribution = -2.0 * scores[:, None, None, :] * projected
        slot_code = nbr_tile // 64
        target_atom = nbr_tile % 64
        ext_x = tile_x + slot_code // 3
        ext_y = tile_y + slot_code % 3
        target = (ext_x * (tiles_y + 2) + ext_y) * 64 + target_atom
        return accumulator.at[target.reshape(-1)].add(
            contribution.reshape(64 * slot_total, 3, sparse_count)
        )

    accumulator = lax.fori_loop(0, tiles_x * tiles_y, add_tile, accumulator)
    extended = accumulator.reshape(tiles_x + 2, tiles_y + 2, 64, 3, sparse_count)
    owned = fold_y(fold_x(extended))
    design = owned.astype(jnp.bfloat16)
    valid_own = valid[0]
    masked = design * valid_own[:, :, :, None, None].astype(jnp.bfloat16)
    masked_rows = masked.reshape(-1, sparse_count)
    force_own = forces[0].astype(jnp.float32)
    local_sumsq = jnp.sum(valid_own[:, :, :, None].astype(jnp.float32) * force_own * force_own)
    group_sumsq = lax.psum(local_sumsq, ("gx", "gy"))
    group_weight = 1.0 / group_sumsq
    gram_part = lax.dot_general(
        masked_rows, masked_rows, (((0,), (0,)), ((), ())), preferred_element_type=jnp.float32
    )
    rhs_part = jnp.dot(forces[0].reshape(-1), masked_rows, preferred_element_type=jnp.float32)
    totals = lax.psum((gram_part * group_weight, rhs_part * group_weight), ("cfg", "gx", "gy"))
    share = sparse_count // lax.axis_size(("gx", "gy"))
    first_row = lax.axis_index(("gx", "gy")) * share
    gram = lax.dynamic_slice_in_dim(totals[0], first_row, share, 0)
    rhs = lax.dynamic_slice_in_dim(totals[1], first_row, share, 0)
    return (design[None], gram, rhs)


def solution(mesh):
    in_specs = (
        P("cfg", "gx", "gy", None, None),
        P("cfg", "gx", "gy", None, None, None, None),
        P("cfg", "gx", "gy", None, None),
        P("cfg", "gx", "gy", None),
        P("cfg", "gx", "gy", None, None),
        P(),
        P(),
    )
    out_specs = (P("cfg", "gx", "gy", None, None, None), P(("gx", "gy"), None), P(("gx", "gy")))
    return jax.shard_map(
        per_device, mesh=mesh, in_specs=in_specs, out_specs=out_specs, check_vma=False
    )
```

profile of v0, /device:TPU:16, one launch (start us, length us, event | category | flops | bytes accessed | tf_op | source)
XLA Modules:
  0.0 1117.1 jit_solution(1140867233260895180)
XLA Ops:
  7.2 0.0 copy-start
  7.2 0.0 all-reduce.2.cloned.1.call-start
  7.2 3.1 copy.28
  10.3 1.4 copy.29
  11.7 0.1 copy.27
  11.8 3.2 gather_fusion
  15.0 0.0 copy-start.5
  15.0 0.0 copy-start.9
  15.0 7.7 broadcast_in_dim.18
  22.7 367.6 %while.20 = (s32[]{:T(128)}, f32[768,3,1024]{2,1,0:T(4,128)}, s32[2,64,16]{2,1,0:T(8,128)S(1)}, bf16[2,64,128]{2,1,0:T(8,128)(2,1)S(1)}, bf16[1024,128]{1,0:T(8,...) while((s32[]{:T(128)}, f32[768,3,1024]{2,1,0:T(4,128)}, ...), condition=%wide.region_2.3_spmd, body=%wide.region_0.2_spmd.sunk | while | flops 828547136 | bytes 105690360 | solution.py:70
  22.7 0.1 squeeze.44
  22.8 0.1 compare_select_fusion.6
  22.9 0.2 fusion.33
  23.1 1.2 constant_dynamic-slice_fusion.7
  24.3 0.4 dot_general.27
  24.7 6.3 broadcast_multiply_fusion.4
  31.0 11.8 %copy.49 = f32[64,16,3,1024]{3,1,0,2:T(8,128)} copy(f32[64,16,3,1024]{3,1,2,0:T(8,128)} %broadcast_multiply_fusion.4) | data formatting | bytes 25165824 | tf_op jit(solution)/shard_map/while/body/eval_jaxpr/mul | solution.py:60
  42.9 18.0 %copy.50 = f32[1024,3,1024]{2,1,0:T(4,128)} copy(f32[1024,3,1024]{2,0,1:T(8,128)} %bitcast.69) | data formatting | bytes 25165824 | tf_op jit(solution)/shard_map/while/body/eval_jaxpr/reshape | solution.py:67
  60.9 145.6 %scatter_fusion = f32[768,3,1024]{2,1,0:T(4,128)} fusion(f32[768,3,1024]{2,1,0:T(4,128)} %get-tuple-element.362, s32[1024]{0:T(1024)S(1)} %bitcast.75, f32[1024,3,1024]{2,1,0:T(4,128)} %copy.50), kind=kCustom, calls=%fused_computation.1.clone.1 | custom fusion | flops 3145728 | bytes 37752832 | tf_op jit(solution)/shard_map/while/body/eval_jaxpr/scatter-add | solution.py:66
  206.5 0.1 squeeze.44
  206.6 0.1 compare_select_fusion.6
  206.7 0.2 fusion.33
  207.0 1.2 constant_dynamic-slice_fusion.7
  208.1 0.4 dot_general.27
  208.6 6.3 broadcast_multiply_fusion.4
  214.9 11.8 %copy.49 = f32[64,16,3,1024]{3,1,0,2:T(8,128)} copy(f32[64,16,3,1024]{3,1,2,0:T(8,128)} %broadcast_multiply_fusion.4) | data formatting | bytes 25165824 | tf_op jit(solution)/shard_map/while/body/eval_jaxpr/mul | solution.py:60
  226.7 18.0 %copy.50 = f32[1024,3,1024]{2,1,0:T(4,128)} copy(f32[1024,3,1024]{2,0,1:T(8,128)} %bitcast.69) | data formatting | bytes 25165824 | tf_op jit(solution)/shard_map/while/body/eval_jaxpr/reshape | solution.py:67
  244.8 145.6 %scatter_fusion = f32[768,3,1024]{2,1,0:T(4,128)} fusion(f32[768,3,1024]{2,1,0:T(4,128)} %get-tuple-element.362, s32[1024]{0:T(1024)S(1)} %bitcast.75, f32[1024,3,1024]{2,1,0:T(4,128)} %copy.50), kind=kCustom, calls=%fused_computation.1.clone.1 | custom fusion | flops 3145728 | bytes 37752832 | tf_op jit(solution)/shard_map/while/body/eval_jaxpr/scatter-add | solution.py:66
  390.3 10.0 copy.30
  400.4 2.9 fusion.17
  403.3 1.6 collective-permute-start
  404.9 0.4 collective-permute-start.1
  405.3 69.2 %collective-permute-done = f32[4,64,3,1024]{3,1,0,2:T(8,128)S(1)} collective-permute-done((f32[4,64,3,1024]{3,1,0,2:T(8,128)}, f32[4,64,3,1024]{3,1,0,2:T(8,128)S(1)}, u32[]{:S(2)}, u32[]{:S(2)}) %collective-permute-start) | collective-permute-done | bytes 3145760 | tf_op jit(solution)/shard_map/ppermute | solution.py:9
  474.5 66.3 %collective-permute-done.1 = f32[4,64,3,1024]{3,1,0,2:T(8,128)S(1)} collective-permute-done((f32[4,64,3,1024]{3,1,0,2:T(8,128)S(1)}, f32[4,64,3,1024]{3,1,0,2:T(8,128)S(1)}, u32[]{:S(2)}, u32[]{:S(2)}) %collective-permute-start.1) | collective-permute-done | bytes 3145760 | tf_op jit(solution)/shard_map/ppermute | solution.py:9
  540.8 1.1 add_bitcast_fusion
  541.9 1.6 copy-done.2
  543.5 1.0 slice_bitcast_fusion
  544.5 4.2 collective-permute-start.2
  548.7 0.0 collective-permute-start.3
  548.8 0.6 fusion.16
  549.4 244.0 %psum.21 = f32[]{:T(128)} all-reduce(f32[]{:T(128)} %fusion.16), channel_id=1, replica_groups=mesh['cfg'=2,'gx'=8,'gy'=16] {'gx','gy'}, use_global_device_ids=true, to_apply=%region_4.5 | all-reduce | flops 1 | bytes 8 | tf_op jit(solution)/shard_map/psum | solution.py:79
  794.0 0.0 slice-start
  794.0 1.4 slice-done
  795.4 0.2 copy.40
  795.6 0.0 collective-permute-done.2
  795.6 0.8 copy-done.3
  796.4 1.2 fusion.13
  797.6 1.3 fusion.11
  799.0 0.2 broadcast_multiply_fusion.1
  799.2 0.0 copy-start.4
  799.2 0.9 copy-done.4
  800.1 3.3 bitcast_multiply_fusion
  803.3 0.0 all-reduce.2.cloned.1.call-update
  803.4 0.1 copy.37
  803.5 0.2 reshape.489
  803.7 0.0 copy-start.1
  803.7 1.9 copy.36
  805.6 1.4 reshape.468
  807.0 1.3 fusion.18
  808.4 111.7 %psum.23 = f32[1024]{0:T(1024)S(1)} all-reduce(f32[1024]{0:T(1024)S(1)} %broadcast_multiply_fusion.2), channel_id=1, replica_groups=mesh['cfg'=2,'gx'=8,'gy'=16] {'cfg','gx','gy'}, use_global_device_ids=true, to_apply=%region_6.7 | all-reduce | flops 1024 | bytes 8192 | tf_op jit(solution)/shard_map/psum | solution.py:85
  920.1 0.6 dynamic_slice.55
  920.7 1.0 convert_bitcast_fusion
  921.7 187.2 %all-reduce.2.cloned.1.call-done = f32[1024,1024]{1,0:T(8,128)} async-done(((f32[1024,1024]{1,0:T(8,128)}), f32[1024,1024]{1,0:T(8,128)}) %all-reduce.2.cloned.1.call-update) | async-done | bytes 4194320 | tf_op jit(solution)/shard_map/psum | solution.py:85
  1108.9 1.4 constant_dynamic-slice_fusion.3
  (20 shorter events, 0.1 us)
Async XLA Ops:
  7.2 4.6 copy-start
  7.2 4.5 copy-start.8
  7.2 4.5 copy-start.6
  7.2 1101.7 %all-reduce.2.cloned.1.call-start = ((), (), s32[]{:S(2)}) async-start(), calls=%async_computation | async-start | bytes 8388608 | tf_op jit(solution)/shard_map/psum | solution.py:85
  15.0 7.7 copy-start.5
  15.0 7.7 copy-start.9
  403.3 71.2 %collective-permute-start = (f32[4,64,3,1024]{3,1,0,2:T(8,128)}, f32[4,64,3,1024]{3,1,0,2:T(8,128)S(1)}, u32[]{:S(2)}, u32[]{:S(2)}) collective-permute-start(f32[4,64,3,1024]{3,1,0,2:T(8,128)} %bitcast.73), channel_id=1, source_target_pairs={{0,112},{16,0},{32,16},{48,32},{64,48},{80,64},{96,80},{112,96},{1... | collective-permute-start | bytes 9437192 | tf_op jit(solution)/shard_map/ppermute | solution.py:9
  404.9 135.9 %collective-permute-start.1 = (f32[4,64,3,1024]{3,1,0,2:T(8,128)S(1)}, f32[4,64,3,1024]{3,1,0,2:T(8,128)S(1)}, u32[]{:S(2)}, u32[]{:S(2)}) collective-permute-start(f32[4,64,3,1024]{3,1,0,2:T(8,128)S(1)} %bitcast.72), channel_id=1, source_target_pairs={{0,16},{16,32},{32,48},{48,64},{64,80},{80,96},{96,112},{112,0},{1... | collective-permute-start | bytes 9437192 | tf_op jit(solution)/shard_map/ppermute | solution.py:9
  541.9 1.6 copy-start.2
  543.5 5.2 copy-start.7
  544.5 251.1 %collective-permute-start.2 = (f32[1,64,3,1024]{3,1,2,0:T(8,128)}, f32[1,64,3,1024]{3,1,2,0:T(8,128)}, u32[]{:S(2)}, u32[]{:S(2)}) collective-permute-start(f32[1,64,3,1024]{3,1,2,0:T(8,128)} %get-tuple-element.304), channel_id=1, source_target_pairs={{0,15},{1,0},{2,1},{3,2},{4,3},{5,4},{6,5},{7,6},{8,7},{9,8},{10,9... | collective-permute-start | bytes 2359304 | tf_op jit(solution)/shard_map/ppermute | solution.py:9
  548.7 248.9 %collective-permute-start.3 = (f32[1,64,3,1024]{3,1,2,0:T(8,128)S(1)}, f32[1,64,3,1024]{3,1,2,0:T(8,128)}, u32[]{:S(2)}, u32[]{:S(2)}) collective-permute-start(f32[1,64,3,1024]{3,1,2,0:T(8,128)S(1)} %get-tuple-element.303), channel_id=1, source_target_pairs={{0,1},{1,2},{2,3},{3,4},{4,5},{5,6},{6,7},{7,8},{8,9},{9,10},{10,1... | collective-permute-start | bytes 2359304 | tf_op jit(solution)/shard_map/ppermute | solution.py:9
  794.0 1.4 slice-start
  794.0 2.4 copy-start.3
  799.2 0.9 copy-start.4
  803.7 306.5 %copy-start.1 = (bf16[2048,128]{1,0:T(8,128)(2,1)S(1)}, bf16[2048,128]{1,0:T(8,128)(2,1)}, u32[]{:S(2)}) copy-start(bf16[2048,128]{1,0:T(8,128)(2,1)} %param.22) | copy-start | bytes 1572868
Sparse Core Ops, SparseCore 0:
  803.5 305.3 all-reduce.1
where the time goes:
time: 1120 us
  blocking collectives  356 us (32%)
  waiting for transfers between devices  323 us (29%)
  other arithmetic  297 us (27%)
  local copies, waits for them, and re-layouts  103 us (9%)
  matrix products  17.7 us (2%)
  between operations  14.9 us (1%)
    scatter-add x2, other arithmetic, add_tile(): accumulator.at[target.reshape(-1)]  291 us
    psum x1, blocking collectives, per_device(): group_sumsq = lax.psum(local_sumsq, ('gx', 'gy'))  244 us
    psum x1, waiting for transfers between devices, per_device(): lax.psum((gram_part * group_weight, rhs_part * group_weight), ('cfg', 'gx...  187 us
    ppermute x4, waiting for transfers between devices, passed_along(): lax.ppermute(x, axis, [(i, (i + by) % length) for i in range(length)])  135 us
    psum x1, blocking collectives, per_device(): lax.psum((gram_part * group_weight, rhs_part * group_weight), ('cfg', 'gx...  112 us
    reshape x2, local copies, waits for them, and re-layouts, add_tile(): contribution.reshape(64 * slot_total, 3, sparse_count)  36.1 us
    mul x2, local copies, waits for them, and re-layouts, add_tile(): contribution = -2.0 * scores[:, None, None, :] * projected  23.7 us
  transfers between devices with their start and end apart: 5, of which 3 were waited for; matrix products, arithmetic and copies ran while one was open for 1% of the time, Pallas kernels for 0%

commit v1 on v0

v1 whole, which is shorter than its diff:
```python
import jax
import jax.numpy as jnp
from jax import lax
from jax.sharding import PartitionSpec as P


def passed_along(x, axis, by):
    length = lax.axis_size(axis)
    return lax.ppermute(x, axis, [(i, (i + by) % length) for i in range(length)])


def fold_x(slab_array):
    inner_count = slab_array.shape[0] - 2
    from_high = passed_along(slab_array[0], "gx", -1)
    from_low = passed_along(slab_array[inner_count + 1], "gx", 1)
    interior = slab_array[1 : inner_count + 1]
    interior = interior.at[inner_count - 1].add(from_high)
    interior = interior.at[0].add(from_low)
    return interior


def fold_y(slab_array):
    inner_count = slab_array.shape[1] - 2
    from_high = passed_along(slab_array[:, 0], "gy", -1)
    from_low = passed_along(slab_array[:, inner_count + 1], "gy", 1)
    interior = slab_array[:, 1 : inner_count + 1]
    interior = interior.at[:, inner_count - 1].add(from_high)
    interior = interior.at[:, 0].add(from_low)
    return interior


def halving_scatter(block, axis):
    length = lax.axis_size(axis)
    index = lax.axis_index(axis)
    distance = length // 2
    while distance >= 1:
        half = block.shape[0] // 2
        lower, upper = block[:half], block[half:]
        upper_side = (index // distance) % 2 == 1
        keep = jnp.where(upper_side, upper, lower)
        send = jnp.where(upper_side, lower, upper)
        pairs = [(i, i ^ distance) for i in range(length)]
        block = keep + lax.ppermute(send, axis, pairs)
        distance //= 2
    return block


def swapped(x, axis):
    length = lax.axis_size(axis)
    return lax.ppermute(x, axis, [(i, i ^ 1) for i in range(length)])


def per_device(descriptors, derivatives, neighbours, valid, forces, pool, sparse_idx):
    tiles_x = descriptors.shape[1]
    tiles_y = descriptors.shape[2]
    tile_count = tiles_x * tiles_y
    slot_total = derivatives.shape[4]
    desc_width = descriptors.shape[4]
    sparse = pool[sparse_idx]
    sparse_count = sparse.shape[0]
    rows = 64 * slot_total
    ext_rows = (tiles_x + 2) * (tiles_y + 2) * 64

    flat_valid = valid.reshape(tile_count, 64)
    flat_desc = descriptors.reshape(tile_count, 64, desc_width)
    flat_desc = jnp.where(flat_valid[:, :, None] != 0, flat_desc, jnp.zeros_like(flat_desc))
    scores = lax.dot_general(
        flat_desc, sparse, (((2,), (1,)), ((), ())), preferred_element_type=jnp.float32
    )
    flat_deriv = derivatives.reshape(tile_count, rows, 3, desc_width)
    projected = lax.dot_general(
        flat_deriv, sparse, (((3,), (1,)), ((), ())), preferred_element_type=jnp.float32
    )
    scores_rep = jnp.repeat(scores, slot_total, axis=1)
    contribution = (-2.0 * scores_rep)[:, :, None, :] * projected
    high_wide = lax.reduce_precision(contribution, exponent_bits=8, mantissa_bits=7)
    high = high_wide.astype(jnp.bfloat16)
    low = (contribution - high_wide).astype(jnp.bfloat16)
    parts = jnp.concatenate([high, low], axis=0).reshape(2 * tile_count, rows, 3 * sparse_count)

    tile_ids = jnp.arange(tile_count, dtype=jnp.int32)
    tile_x = (tile_ids // tiles_y)[:, None]
    tile_y = (tile_ids % tiles_y)[:, None]
    flat_nbr = neighbours.reshape(tile_count, rows)
    slot_code = flat_nbr // 64
    target_atom = flat_nbr % 64
    ext_x = tile_x + slot_code // 3
    ext_y = tile_y + slot_code % 3
    target = (ext_x * (tiles_y + 2) + ext_y) * 64 + target_atom
    onehot = (
        jnp.arange(ext_rows, dtype=jnp.int32)[None, :, None] == target[:, None, :]
    ).astype(jnp.bfloat16)
    onehot = jnp.concatenate([onehot, onehot], axis=0)
    accumulator = lax.dot_general(
        onehot, parts, (((0, 2), (0, 1)), ((), ())), preferred_element_type=jnp.float32
    )
    extended = accumulator.reshape(tiles_x + 2, tiles_y + 2, 64, 3, sparse_count)
    owned = fold_x(fold_y(extended))
    design = owned.astype(jnp.bfloat16)

    valid_own = valid[0]
    masked = design * valid_own[:, :, :, None, None].astype(jnp.bfloat16)
    masked_rows = masked.reshape(-1, sparse_count)
    force_own = forces[0].astype(jnp.float32)
    local_sumsq = jnp.sum(valid_own[:, :, :, None].astype(jnp.float32) * force_own * force_own)
    gram_part = lax.dot_general(
        masked_rows, masked_rows, (((0,), (0,)), ((), ())), preferred_element_type=jnp.float32
    )
    rhs_part = jnp.dot(forces[0].reshape(-1), masked_rows, preferred_element_type=jnp.float32)

    pad_cols = 128
    extra = jnp.zeros((sparse_count, pad_cols), jnp.float32)
    extra = extra.at[:, 0].set(rhs_part).at[:, 1].set(local_sumsq)
    packed = jnp.concatenate([gram_part, extra], axis=1)
    gx_size = lax.axis_size("gx")
    gy_size = lax.axis_size("gy")
    packed = packed.reshape(gx_size, gy_size, -1, packed.shape[1]).swapaxes(0, 1)
    packed = packed.reshape(sparse_count, -1)
    reduced = lax.psum_scatter(packed, "gy", scatter_dimension=0, tiled=True)
    reduced = halving_scatter(reduced, "gx")
    weighted = reduced / reduced[:, sparse_count + 1 : sparse_count + 2]
    total = weighted + swapped(weighted, "cfg")
    gram = total[:, :sparse_count]
    rhs = total[:, sparse_count]
    return (design[None], gram, rhs)


def solution(mesh):
    in_specs = (
        P("cfg", "gx", "gy", None, None),
        P("cfg", "gx", "gy", None, None, None, None),
        P("cfg", "gx", "gy", None, None),
        P("cfg", "gx", "gy", None),
        P("cfg", "gx", "gy", None, None),
        P(),
        P(),
    )
    out_specs = (P("cfg", "gx", "gy", None, None, None), P(("gx", "gy"), None), P(("gx", "gy")))
    return jax.shard_map(
        per_device, mesh=mesh, in_specs=in_specs, out_specs=out_specs, check_vma=False
    )
```

time: 1120 us -> 302 us (0.27)
  blocking collectives: 356 us -> 0 us
  other arithmetic: 297 us -> 19.7 us
  waiting for transfers between devices: 323 us -> 167 us
  local copies, waits for them, and re-layouts: 103 us -> 43 us
  matrix products: 17.7 us -> 42.7 us
    psum x2 -> x0, blocking collectives: 356 us -> none  [the longest x1 244 us: per_device(): group_sumsq = lax.psum(local_sumsq, ('gx', 'gy'))]
    scatter-add x3 -> x0, other arithmetic: 292 us -> none  [the longest x2 291 us: add_tile(): accumulator.at[target.reshape(-1)]]
    psum x1 -> x0, waiting for transfers between devices: 187 us -> none  [per_device(): lax.psum((gram_part * group_weight, rhs_part * group_weight), ('cfg', 'gx...]
    reduce_scatter x0 -> x1, waiting for transfers between devices: none -> 66.8 us  [per_device(): reduced = lax.psum_scatter(packed, 'gy', scatter_dimension=0, tiled=True)]
    ppermute x4, waiting for transfers between devices: 135 us -> 85.2 us  [passed_along(): lax.ppermute(x, axis, [(i, (i + by) % length) for i in range(length)])]
    reshape x2 -> x1, local copies, waits for them, and re-layouts: 36.1 us -> 0.09 us  [per_device(): flat_nbr = neighbours.reshape(tile_count, rows)]
    dot_general x4 -> x3, matrix products: 13.1 us -> 39.1 us  [the longest x1 25.6 us: per_device(): lax.dot_general(onehot, parts, (((0, 2), (0, 1)), ((), ())), preferred_el...]
    ppermute x0 -> x4, waiting for transfers between devices: none -> 15.2 us  [the longest x3 12.7 us: halving_scatter(): block = keep + lax.ppermute(send, axis, pairs)]
  transfers between devices with their start and end apart: 5 -> 9, of which waited for: 3 -> 9; matrix products, arithmetic and copies ran while one was open for 1% -> 1% of each run, Pallas kernels for 0% -> 0%
where the time goes in v1:
time: 302 us
  waiting for transfers between devices  167 us (55%)
  local copies, waits for them, and re-layouts  43 us (14%)
  matrix products  42.7 us (14%)
  other arithmetic  19.7 us (7%)
  between operations  15.6 us (5%)
  starting transfers between devices  13.7 us (5%)
    ppermute x4, waiting for transfers between devices, passed_along(): lax.ppermute(x, axis, [(i, (i + by) % length) for i in range(length)])  85.2 us
    reduce_scatter x1, waiting for transfers between devices, per_device(): reduced = lax.psum_scatter(packed, 'gy', scatter_dimension=0, tiled=True)  66.8 us
    dot_general x1, matrix products, per_device(): lax.dot_general(onehot, parts, (((0, 2), (0, 1)), ((), ())), preferred_el...  25.6 us
    ppermute x3, waiting for transfers between devices, halving_scatter(): block = keep + lax.ppermute(send, axis, pairs)  12.7 us
    dot_general x1, matrix products, per_device(): lax.dot_general(flat_deriv, sparse, (((3,), (1,)), ((), ())), preferred_e...  12.5 us
    mul x1, local copies, waits for them, and re-layouts, per_device(): contribution = (-2.0 * scores_rep)[:, :, None, :] * projected  8.69 us
    ppermute x4, starting transfers between devices, passed_along(): lax.ppermute(x, axis, [(i, (i + by) % length) for i in range(length)])  7.35 us
    concatenate x1, local copies, waits for them, and re-layouts, per_device(): packed = jnp.concatenate([gram_part, extra], axis=1)  6.18 us
  transfers between devices with their start and end apart: 9, of which 9 were waited for; matrix products, arithmetic and copies ran while one was open for 1% of the time, Pallas kernels for 0%

profile of v1, /device:TPU:16, one launch (start us, length us, event | category | flops | bytes accessed | tf_op | source)
XLA Modules:
  0.0 301.8 jit_solution(12376506824223177642)
XLA Ops:
  7.2 0.0 copy-start
  7.2 0.0 reduce-scatter.2.cloned.1.call-start
  7.2 0.7 fusion.24
  8.0 0.7 compare_bitcast_fusion
  8.7 3.2 %gather_fusion = bf16[1024,128]{1,0:T(8,128)(2,1)S(1)} fusion(bf16[2048,128]{1,0:T(8,128)(2,1)S(1)} %copy-done, s32[1024]{0:T(1024)S(1)} %fusion.24), kind=kCustom, calls=%fused_computation | custom fusion | bytes 528384 | tf_op jit(solution)/shard_map/gather | solution.py:59
  11.9 1.0 convolution_multiply_fusion
  12.9 4.3 %broadcast_in_dim.30 = f32[2,64,16,1024]{3,2,1,0:T(8,128)} broadcast(f32[2,64,1024]{2,1,0:T(8,128)S(1)} %convolution_multiply_fusion), dimensions={0,1,3} | broadcast | bytes 8912896 | tf_op jit(solution)/shard_map/broadcast_in_dim | solution.py:74
  17.2 8.7 %copy.45 = f32[2,1024,1024]{1,2,0:T(8,128)} copy(f32[2,1024,1024]{2,1,0:T(8,128)} %bitcast.106) | data formatting | bytes 16777216 | tf_op jit(solution)/shard_map/mul | solution.py:75
  25.9 1.7 copy.46
  27.6 0.0 copy-done.4
  27.6 0.1 copy.44
  27.7 0.1 reshape.410
  27.8 0.1 fusion.23
  27.9 0.9 iota_compare_fusion
  28.8 2.7 pad_add_fusion
  31.6 12.5 %reduce-precision_convert_fusion = (bf16[2,1024,3,1024]{1,3,2,0:T(8,128)(2,1)}, bf16[2,1024,3,1024]{1,3,2,0:T(8,128)(2,1)}) fusion(f32[2,1024,1024]{1,2,0:T(8,128)} %copy.45, bf16[2,1024,3,128]{3,1,2,0:T(8,128)(2,1)S(1)} %bitcast.109, bf16[1024,128]{1,0:T(8,128)(2,1)S(1)} %gather_fusion), kind=kOutput, calls=%fused_computation.2 | convolution fusion | flops 1642070016 | bytes 35389440 | tf_op jit(solution)/shard_map/dot_general | solution.py:71
  44.1 25.6 %fusion.4 = f32[3,4,64,3,1024]{4,2,3,1,0:T(8,128)} fusion(pred[3,4,64,4,1024,1]{4,2,1,0,3,5:T(32,128)(4,1)} %bitcast.110, bf16[2,1024,3,1024]{1,3,2,0:T(8,128)(2,1)} %get-tuple-element.78, bf16[2,1024,3,1024]{1,3,2,0:T(8,128)(2,1)} %get-tuple-element.77), kind=kOutput, calls=%fused_computation.12 | convolution fusion | flops 19339935744 | bytes 37748736 | tf_op jit(solution)/shard_map/dot_general | solution.py:94
  69.7 3.1 %slice_bitcast_fusion = (f32[3,64,3,1024]{3,1,2,0:T(8,128)S(1)}, f32[3,64,3,1024]{3,1,2,0:T(8,128)S(1)}) fusion(f32[3,4,64,3,1024]{4,2,3,1,0:T(8,128)} %fusion.4), kind=kLoop, calls=%fused_computation.13 | loop fusion | bytes 9437184 | tf_op jit(solution)/shard_map/squeeze | solution.py:25
  72.8 5.3 %collective-permute-start = (f32[3,64,3,1024]{3,1,2,0:T(8,128)S(1)}, f32[3,64,3,1024]{3,1,2,0:T(8,128)S(1)}, u32[]{:S(2)}, u32[]{:S(2)}) collective-permute-start(f32[3,64,3,1024]{3,1,2,0:T(8,128)S(1)} %get-tuple-element.80), channel_id=1, source_target_pairs={{0,15},{1,0},{2,1},{3,2},{4,3},{5,4},{6,5},{7,6},{8,7},{9,8},{10,9... | collective-permute-start | bytes 7077896 | tf_op jit(solution)/shard_map/ppermute | solution.py:9
  78.1 0.0 collective-permute-start.1
  78.1 2.3 slice-done
  80.4 0.7 copy.67
  81.1 23.3 %collective-permute-done = f32[3,64,3,1024]{3,1,2,0:T(8,128)S(1)} collective-permute-done((f32[3,64,3,1024]{3,1,2,0:T(8,128)S(1)}, f32[3,64,3,1024]{3,1,2,0:T(8,128)S(1)}, u32[]{:S(2)}, u32[]{:S(2)}) %collective-permute-start) | collective-permute-done | bytes 2359328 | tf_op jit(solution)/shard_map/ppermute | solution.py:9
  104.4 0.7 fusion.11
  105.1 2.5 collective-permute-done.1
  107.6 0.8 fusion.9
  108.4 2.1 copy-done.2
  110.5 2.1 slice_bitcast_fusion.4
  112.6 1.4 collective-permute-start.2
  114.0 0.7 collective-permute-start.3
  114.6 0.1 copy.55
  114.8 0.2 reshape.439
  115.0 0.6 compare_reduce_fusion
  115.6 0.6 fusion.25
  117.5 0.6 compare_reduce_fusion.1
  118.2 31.9 %collective-permute-done.2 = f32[2,64,3,1024]{3,1,2,0:T(8,128)S(1)} collective-permute-done((f32[2,64,3,1024]{3,1,2,0:T(8,128)}, f32[2,64,3,1024]{3,1,2,0:T(8,128)S(1)}, u32[]{:S(2)}, u32[]{:S(2)}) %collective-permute-start.2) | collective-permute-done | bytes 1572896 | tf_op jit(solution)/shard_map/ppermute | solution.py:9
  150.1 27.5 %collective-permute-done.3 = f32[2,64,3,1024]{3,1,2,0:T(8,128)} collective-permute-done((f32[2,64,3,1024]{3,1,2,0:T(8,128)}, f32[2,64,3,1024]{3,1,2,0:T(8,128)}, u32[]{:S(2)}, u32[]{:S(2)}) %collective-permute-start.3) | collective-permute-done | bytes 1572896 | tf_op jit(solution)/shard_map/ppermute | solution.py:9
  177.6 3.3 %broadcast_multiply_fusion = (bf16[1,2,64,3,1024]{4,2,3,1,0:T(8,128)(2,1)S(1)}, bf16[1,2,64,3,1024]{4,2,3,1,0:T(8,128)(2,1)}) fusion(bf16[2,64]{1,0:T(2,128)(2,1)S(1)} %get-tuple-element.84, f32[2,64,3,1024]{3,1,2,0:T(8,128)} %collective-permute-done.3, f32[2,64,3,1024]{3,1,2,0:T(8,128)S(1)} %collective-permute-done.2, f32[3,2,64,3,1024]{4,2,3,0,1:T(8,128)} %copy-done.2), kind=kLoop, calls=%fused_computation.29 | loop fusion | flops 1572864 | bytes 6291712 | tf_op jit(solution)/shard_map/mul | solution.py:102
  180.9 0.7 copy.54
  181.6 3.3 %convolution_bitcast_fusion = f32[1024,1024]{0,1:T(8,128)} fusion(bf16[1,2,64,3,1024]{4,2,3,1,0:T(8,128)(2,1)S(1)} %get-tuple-element.75), kind=kOutput, calls=%fused_computation.20 | convolution fusion | flops 805306368 | bytes 4980736 | tf_op jit(solution)/shard_map/dot_general | solution.py:106
  184.9 0.7 reshape.419
  185.6 0.2 fusion.28
  185.8 0.7 broadcast_select_fusion
  186.5 0.1 scatter.9
  186.6 5.0 %pad_maximum_fusion = f32[1024,1152]{0,1:T(8,128)} fusion(f32[1024,128]{0,1:T(8,128)S(1)} %scatter.9, f32[1024,1024]{0,1:T(8,128)} %convolution_bitcast_fusion), kind=kLoop, calls=%fused_computation.11 | loop fusion | flops 1179648 | bytes 9437184 | tf_op jit(solution)/shard_map/concatenate | solution.py:114
  191.7 6.2 %copy.56 = f32[1024,1152]{1,0:T(8,128)} copy(f32[1024,1152]{0,1:T(8,128)} %pad_maximum_fusion) | data formatting | bytes 9437184 | tf_op jit(solution)/shard_map/concatenate | solution.py:114
  197.9 5.0 %copy.57 = f32[16,8,8,1152]{3,2,1,0:T(8,128)} copy(f32[16,8,8,1152]{3,2,0,1:T(8,128)} %bitcast.108) | data formatting | bytes 9437184 | tf_op jit(solution)/shard_map/transpose | solution.py:117
  202.9 0.0 reduce-scatter.2.cloned.1.call-update
  202.9 66.8 %reduce-scatter.2.cloned.1.call-done = f32[64,1152]{1,0:T(8,128)} async-done(((f32[1024,1152]{1,0:T(8,128)}), f32[64,1152]{1,0:T(8,128)}) %reduce-scatter.2.cloned.1.call-update) | async-done | bytes 294928 | tf_op jit(solution)/shard_map/reduce_scatter | solution.py:119
  269.8 1.0 slice_select_fusion
  270.8 0.6 collective-permute-start.4
  271.3 6.9 %collective-permute-done.4 = f32[32,1152]{1,0:T(8,128)S(1)} collective-permute-done((f32[32,1152]{1,0:T(8,128)S(1)}, f32[32,1152]{1,0:T(8,128)S(1)}, u32[]{:S(2)}, u32[]{:S(2)}) %collective-permute-start.4) | collective-permute-done | bytes 147488 | tf_op jit(solution)/shard_map/ppermute | solution.py:43
  278.3 1.0 select_add_fusion
  279.3 1.2 collective-permute-start.5
  280.5 3.2 %collective-permute-done.5 = f32[16,1152]{1,0:T(8,128)S(1)} collective-permute-done((f32[16,1152]{1,0:T(8,128)S(1)}, f32[16,1152]{1,0:T(8,128)S(1)}, u32[]{:S(2)}, u32[]{:S(2)}) %collective-permute-start.5) | collective-permute-done | bytes 73760 | tf_op jit(solution)/shard_map/ppermute | solution.py:43
  283.8 1.5 collective-permute-start.6
  285.3 2.5 collective-permute-done.6
  287.8 0.2 slice_reduce_fusion.1
  288.0 0.1 broadcast_divide_fusion
  288.1 3.0 collective-permute-start.7
  291.1 2.5 collective-permute-done.7
  293.6 0.1 fusion.32
  293.7 0.6 slice.231
  294.3 0.6 slice_reduce_fusion
  (20 shorter events, 0.1 us)
Async XLA Ops:
  7.2 1.5 copy-start
  7.2 262.6 %reduce-scatter.2.cloned.1.call-start = ((), (), s32[]{:S(2)}) async-start(), calls=%async_computation.1 | async-start | bytes 5013504 | tf_op jit(solution)/shard_map/reduce_scatter | solution.py:119
  17.2 10.4 %copy-start.4 = (s32[1,1,2,64,16]{3,4,2,1,0:T(8,128)S(1)}, s32[1,1,2,64,16]{3,4,2,1,0:T(8,128)}, u32[]{:S(2)}) copy-start(s32[1,1,2,64,16]{3,4,2,1,0:T(8,128)} %param.21) | copy-start | bytes 24580
  72.8 31.7 %collective-permute-start = (f32[3,64,3,1024]{3,1,2,0:T(8,128)S(1)}, f32[3,64,3,1024]{3,1,2,0:T(8,128)S(1)}, u32[]{:S(2)}, u32[]{:S(2)}) collective-permute-start(f32[3,64,3,1024]{3,1,2,0:T(8,128)S(1)} %get-tuple-element.80), channel_id=1, source_target_pairs={{0,15},{1,0},{2,1},{3,2},{4,3},{5,4},{6,5},{7,6},{8,7},{9,8},{10,9... | collective-permute-start | bytes 7077896 | tf_op jit(solution)/shard_map/ppermute | solution.py:9
  78.1 2.3 slice-start
  78.1 29.5 %collective-permute-start.1 = (f32[3,64,3,1024]{3,1,2,0:T(8,128)S(1)}, f32[3,64,3,1024]{3,1,2,0:T(8,128)S(1)}, u32[]{:S(2)}, u32[]{:S(2)}) collective-permute-start(f32[3,64,3,1024]{3,1,2,0:T(8,128)S(1)} %get-tuple-element.79), channel_id=1, source_target_pairs={{0,1},{1,2},{2,3},{3,4},{4,5},{5,6},{6,7},{7,8},{8,9},{9,10},{10,1... | collective-permute-start | bytes 7077896 | tf_op jit(solution)/shard_map/ppermute | solution.py:9
  80.4 24.0 %copy-start.3 = (f32[3,4,64,3,1024]{4,2,3,1,0:T(8,128)S(1)}, f32[3,4,64,3,1024]{4,2,3,1,0:T(8,128)}, u32[]{:S(2)}) copy-start(f32[3,4,64,3,1024]{4,2,3,1,0:T(8,128)} %fusion.4) | copy-start | bytes 28311556
  108.3 2.1 copy-start.2
  110.5 4.2 %copy-start.5 = (bf16[1,1,2,64,3]{3,2,4,1,0:T(2,128)(2,1)S(1)}, bf16[1,1,2,64,3]{3,2,4,1,0:T(2,128)(2,1)}, u32[]{:S(2)}) copy-start(bf16[1,1,2,64,3]{3,2,4,1,0:T(2,128)(2,1)} %param.23) | copy-start | bytes 2308
  110.5 5.1 %copy-start.6 = (s32[1,1,2,64]{3,2,1,0:T(2,128)S(1)}, s32[1,1,2,64]{3,2,1,0:T(2,128)}, u32[]{:S(2)}) copy-start(s32[1,1,2,64]{3,2,1,0:T(2,128)} %param.22) | copy-start | bytes 1540
  112.6 37.5 %collective-permute-start.2 = (f32[2,64,3,1024]{3,1,2,0:T(8,128)}, f32[2,64,3,1024]{3,1,2,0:T(8,128)S(1)}, u32[]{:S(2)}, u32[]{:S(2)}) collective-permute-start(f32[2,64,3,1024]{3,1,2,0:T(8,128)} %get-tuple-element.81), channel_id=1, source_target_pairs={{0,112},{16,0},{32,16},{48,32},{64,48},{80,64},{96,80},{112,96},{1... | collective-permute-start | bytes 4718600 | tf_op jit(solution)/shard_map/ppermute | solution.py:9
  114.0 63.6 %collective-permute-start.3 = (f32[2,64,3,1024]{3,1,2,0:T(8,128)}, f32[2,64,3,1024]{3,1,2,0:T(8,128)}, u32[]{:S(2)}, u32[]{:S(2)}) collective-permute-start(f32[2,64,3,1024]{3,1,2,0:T(8,128)} %get-tuple-element.82), channel_id=1, source_target_pairs={{0,16},{16,32},{32,48},{48,64},{64,80},{80,96},{96,112},{112,0},{1... | collective-permute-start | bytes 4718600 | tf_op jit(solution)/shard_map/ppermute | solution.py:9
  197.9 97.0 %copy-start.1 = (bf16[2048,128]{1,0:T(8,128)(2,1)S(1)}, bf16[2048,128]{1,0:T(8,128)(2,1)}, u32[]{:S(2)}) copy-start(bf16[2048,128]{1,0:T(8,128)(2,1)} %param.24) | copy-start | bytes 1572868
  270.8 7.5 %collective-permute-start.4 = (f32[32,1152]{1,0:T(8,128)S(1)}, f32[32,1152]{1,0:T(8,128)S(1)}, u32[]{:S(2)}, u32[]{:S(2)}) collective-permute-start(f32[32,1152]{1,0:T(8,128)S(1)} %slice_select_fusion), channel_id=1, source_target_pairs={{0,64},{16,80},{32,96},{48,112},{64,0},{80,16},{96,32},{112,48},{1... | collective-permute-start | bytes 442376 | tf_op jit(solution)/shard_map/ppermute | solution.py:43
  279.3 4.4 %collective-permute-start.5 = (f32[16,1152]{1,0:T(8,128)S(1)}, f32[16,1152]{1,0:T(8,128)S(1)}, u32[]{:S(2)}, u32[]{:S(2)}) collective-permute-start(f32[16,1152]{1,0:T(8,128)S(1)} %slice_select_fusion.1), channel_id=1, source_target_pairs={{0,32},{16,48},{32,0},{48,16},{64,96},{80,112},{96,64},{112,80},{1... | collective-permute-start | bytes 221192 | tf_op jit(solution)/shard_map/ppermute | solution.py:43
  283.8 4.0 %collective-permute-start.6 = (f32[8,1152]{1,0:T(8,128)S(1)}, f32[8,1152]{1,0:T(8,128)S(1)}, u32[]{:S(2)}, u32[]{:S(2)}) collective-permute-start(f32[8,1152]{1,0:T(8,128)S(1)} %slice_select_fusion.2), channel_id=1, source_target_pairs={{0,16},{16,0},{32,48},{48,32},{64,80},{80,64},{96,112},{112,96},{1... | collective-permute-start | bytes 110600 | tf_op jit(solution)/shard_map/ppermute | solution.py:43
  288.1 5.5 %collective-permute-start.7 = (f32[8,1152]{1,0:T(8,128)S(1)}, f32[8,1152]{1,0:T(8,128)S(1)}, u32[]{:S(2)}, u32[]{:S(2)}) collective-permute-start(f32[8,1152]{1,0:T(8,128)S(1)} %broadcast_divide_fusion), channel_id=1, source_target_pairs={{0,128},{128,0},{1,129},{129,1},{2,130},{130,2},{3,131},{131,3},{4... | collective-permute-start | bytes 110600 | tf_op jit(solution)/shard_map/ppermute | solution.py:50
Sparse Core Ops, SparseCore 0:
  203.0 66.6 reduce-scatter.1

commit v2 on v1

--- a/solution.py
+++ b/solution.py
@@ -1,4 +1,5 @@
 import jax
+import numpy as np
 import jax.numpy as jnp
 from jax import lax
 from jax.sharding import PartitionSpec as P
@@ -86,36 +87,66 @@
     target_atom = flat_nbr % 64
     ext_x = tile_x + slot_code // 3
     ext_y = tile_y + slot_code % 3
-    target = (ext_x * (tiles_y + 2) + ext_y) * 64 + target_atom
-    onehot = (
-        jnp.arange(ext_rows, dtype=jnp.int32)[None, :, None] == target[:, None, :]
-    ).astype(jnp.bfloat16)
-    onehot = jnp.concatenate([onehot, onehot], axis=0)
-    accumulator = lax.dot_general(
-        onehot, parts, (((0, 2), (0, 1)), ((), ())), preferred_element_type=jnp.float32
-    )
-    extended = accumulator.reshape(tiles_x + 2, tiles_y + 2, 64, 3, sparse_count)
-    owned = fold_x(fold_y(extended))
-    design = owned.astype(jnp.bfloat16)
+    target_tile = ext_x * (tiles_y + 2) + ext_y
+
+    def gathered(tiles):
+        lookup = np.full((tiles_x + 2) * (tiles_y + 2), -1, np.int32)
+        for place, (x, y) in enumerate(tiles):
+            lookup[x * (tiles_y + 2) + y] = place
+        key = jnp.asarray(lookup)[target_tile] * 64 + target_atom
+        onehot = (
+            jnp.arange(len(tiles) * 64, dtype=jnp.int32)[None, :, None] == key[:, None, :]
+        ).astype(jnp.bfloat16)
+        onehot = jnp.concatenate([onehot, onehot], axis=0)
+        summed = lax.dot_general(
+            onehot, parts, (((0, 2), (0, 1)), ((), ())), preferred_element_type=jnp.float32
+        )
+        return summed.reshape(len(tiles), 64, 3, sparse_count)
+
+    ext_cols = range(tiles_x + 2)
+    edge_y = gathered([(x, 0) for x in ext_cols] + [(x, tiles_y + 1) for x in ext_cols])
+    edge_y = edge_y.reshape(2, tiles_x + 2, 64, 3, sparse_count)
+    from_high_y = passed_along(edge_y[0], "gy", -1)
+    from_low_y = passed_along(edge_y[1], "gy", 1)
+    inner_y = range(1, tiles_y + 1)
+    edge_x = gathered([(0, y) for y in inner_y] + [(tiles_x + 1, y) for y in inner_y])
+    edge_x = edge_x.reshape(2, tiles_y, 64, 3, sparse_count)
+    own = gathered([(x, y) for x in range(1, tiles_x + 1) for y in inner_y])
+    own = own.reshape(tiles_x, tiles_y, 64, 3, sparse_count)
+    edge_x = edge_x.at[:, tiles_y - 1].add(from_high_y[:: tiles_x + 1])
+    edge_x = edge_x.at[:, 0].add(from_low_y[:: tiles_x + 1])
+    from_high_x = passed_along(edge_x[0], "gx", -1)
+    from_low_x = passed_along(edge_x[1], "gx", 1)
+    own = own.at[:, tiles_y - 1].add(from_high_y[1 : tiles_x + 1])
+    own = own.at[:, 0].add(from_low_y[1 : tiles_x + 1])
+    own = own.at[tiles_x - 1].add(from_high_x)
+    own = own.at[0].add(from_low_x)
+    design = own.astype(jnp.bfloat16)
 
     valid_own = valid[0]
     masked = design * valid_own[:, :, :, None, None].astype(jnp.bfloat16)
     masked_rows = masked.reshape(-1, sparse_count)
     force_own = forces[0].astype(jnp.float32)
     local_sumsq = jnp.sum(valid_own[:, :, :, None].astype(jnp.float32) * force_own * force_own)
-    gram_part = lax.dot_general(
-        masked_rows, masked_rows, (((0,), (0,)), ((), ())), preferred_element_type=jnp.float32
-    )
-    rhs_part = jnp.dot(forces[0].reshape(-1), masked_rows, preferred_element_type=jnp.float32)
 
-    pad_cols = 128
-    extra = jnp.zeros((sparse_count, pad_cols), jnp.float32)
-    extra = extra.at[:, 0].set(rhs_part).at[:, 1].set(local_sumsq)
-    packed = jnp.concatenate([gram_part, extra], axis=1)
     gx_size = lax.axis_size("gx")
     gy_size = lax.axis_size("gy")
-    packed = packed.reshape(gx_size, gy_size, -1, packed.shape[1]).swapaxes(0, 1)
-    packed = packed.reshape(sparse_count, -1)
+    share = sparse_count // (gx_size * gy_size)
+    pad_cols = 128
+    reordered = masked_rows.reshape(-1, gx_size, gy_size, share).swapaxes(1, 2)
+    reordered = reordered.reshape(-1, sparse_count)
+    right = jnp.concatenate(
+        [
+            masked_rows,
+            forces[0].reshape(-1, 1),
+            jnp.zeros((masked_rows.shape[0], pad_cols - 1), jnp.bfloat16),
+        ],
+        axis=1,
+    )
+    packed = lax.dot_general(
+        reordered, right, (((0,), (0,)), ((), ())), preferred_element_type=jnp.float32
+    )
+    packed = packed.at[:, sparse_count + 1].set(local_sumsq)
     reduced = lax.psum_scatter(packed, "gy", scatter_dimension=0, tiled=True)
     reduced = halving_scatter(reduced, "gx")
     weighted = reduced / reduced[:, sparse_count + 1 : sparse_count + 2]

time: 302 us -> 393 us (1.30)
  local copies, waits for them, and re-layouts: 43 us -> 119 us
  other arithmetic: 19.7 us -> 53.3 us
  waiting for transfers between devices: 167 us -> 135 us
  matrix products: 42.7 us -> 55.7 us
    gather x0 -> x3, local copies, waits for them, and re-layouts: none -> 37.9 us  [gathered(): key = jnp.asarray(lookup)[target_tile] * 64 + target_atom]
    ppermute x4, waiting for transfers between devices: 85.2 us -> 52.8 us  [passed_along(): lax.ppermute(x, axis, [(i, (i + by) % length) for i in range(length)])]
    dot_general x0 -> x1, other arithmetic: none -> 31.5 us  [gathered(): lax.dot_general(onehot, parts, (((0, 2), (0, 1)), ((), ())), preferred_el...]
    squeeze x2 -> x5, local copies, waits for them, and re-layouts: 5.21 us -> 21.2 us  [the longest x2 9.41 us: per_device(): from_high_y = passed_along(edge_y[0], 'gy', -1)]
    another operation x2, local copies, waits for them, and re-layouts: 0.22 us -> 15.7 us  [the longest x1 15.6 us: per_device(): reordered = masked_rows.reshape(-1, gx_size, gy_size, share).swapaxes(1, 2)]
    dot_general x3 -> x4, matrix products: 29.1 us -> 42.1 us  [the longest x3 40.7 us: gathered(): lax.dot_general(onehot, parts, (((0, 2), (0, 1)), ((), ())), preferred_el...]
    transpose x1, local copies, waits for them, and re-layouts: 5 us -> 14.3 us  [per_device(): reordered = masked_rows.reshape(-1, gx_size, gy_size, share).swapaxes(1, 2)]
    scatter-add x2 -> x4, other arithmetic: 1.43 us -> 9.85 us  [the longest x1 3.65 us: per_device(): edge_x = edge_x.at[:, 0].add(from_low_y[::tiles_x + 1])]
  transfers between devices with their start and end apart: 9 -> 9, of which waited for: 9 -> 9; matrix products, arithmetic and copies ran while one was open for 1% -> 12% of each run, Pallas kernels for 0% -> 0%
where the time goes in v2:
time: 393 us; the launch traced here: 392 us
  waiting for transfers between devices  135 us (34%)
  local copies, waits for them, and re-layouts  119 us (30%)
  matrix products  55.7 us (14%)
  other arithmetic  53.3 us (14%)
  starting transfers between devices  14.7 us (4%)
  between operations  14.4 us (4%)
    reduce_scatter x1, waiting for transfers between devices, per_device(): reduced = lax.psum_scatter(packed, 'gy', scatter_dimension=0, tiled=True)  66.7 us
    ppermute x4, waiting for transfers between devices, passed_along(): lax.ppermute(x, axis, [(i, (i + by) % length) for i in range(length)])  52.8 us
    dot_general x3, matrix products, gathered(): lax.dot_general(onehot, parts, (((0, 2), (0, 1)), ((), ())), preferred_el...  40.7 us
    gather x3, local copies, waits for them, and re-layouts, gathered(): key = jnp.asarray(lookup)[target_tile] * 64 + target_atom  37.9 us
    dot_general x1, other arithmetic, gathered(): lax.dot_general(onehot, parts, (((0, 2), (0, 1)), ((), ())), preferred_el...  31.5 us
    another operation x1, local copies, waits for them, and re-layouts, per_device(): reordered = masked_rows.reshape(-1, gx_size, gy_size, share).swapaxes(1, 2)  15.6 us
    transpose x1, local copies, waits for them, and re-layouts, per_device(): reordered = masked_rows.reshape(-1, gx_size, gy_size, share).swapaxes(1, 2)  14.3 us
    ppermute x3, waiting for transfers between devices, halving_scatter(): block = keep + lax.ppermute(send, axis, pairs)  12.6 us
  transfers between devices with their start and end apart: 9, of which 9 were waited for; matrix products, arithmetic and copies ran while one was open for 12% of the time, Pallas kernels for 0%

profile of v2, /device:TPU:16, one launch (start us, length us, event | category | flops | bytes accessed | tf_op | source)
XLA Modules:
  0.0 391.8 jit_solution(15298467509881458007)
XLA Ops:
  7.2 0.8 copy.17
  8.3 0.7 fusion.38
  9.0 0.7 compare_bitcast_fusion
  9.7 3.2 gather_fusion.1
  12.9 1.0 convolution_multiply_fusion
  13.9 4.3 %broadcast_in_dim.21 = f32[2,64,16,1024]{3,2,1,0:T(8,128)} broadcast(f32[2,64,1024]{2,1,0:T(8,128)S(1)} %convolution_multiply_fusion), dimensions={0,1,3} | broadcast | bytes 8912896 | tf_op jit(solution)/shard_map/broadcast_in_dim | solution.py:75
  18.2 8.7 %copy.19 = f32[2,1024,1024]{1,2,0:T(8,128)} copy(f32[2,1024,1024]{2,1,0:T(8,128)} %bitcast.119) | data formatting | bytes 16777216 | tf_op jit(solution)/shard_map/mul | solution.py:76
  27.0 1.7 copy.20
  28.8 12.6 %gather_fusion.2 = s32[2048]{0:T(1024)S(1)} fusion(s32[12]{0:T(128)S(1)} %copy-done.3, s32[2048]{0:T(1024)S(1)} %bitcast_clamp_fusion), kind=kCustom, calls=%fused_computation.2 | custom fusion | bytes 24576 | tf_op jit(solution)/shard_map/gather | solution.py:96
  41.4 12.6 %gather_fusion = s32[2048]{0:T(1024)S(1)} fusion(s32[12]{0:T(128)S(1)} %copy-done.4, s32[2048]{0:T(1024)S(1)} %bitcast_clamp_fusion), kind=kCustom, calls=%fused_computation | custom fusion | bytes 24576 | tf_op jit(solution)/shard_map/gather | solution.py:96
  54.1 12.6 %gather_fusion.3 = s32[2048]{0:T(1024)S(1)} fusion(s32[12]{0:T(128)S(1)} %copy-done.2, s32[2048]{0:T(1024)S(1)} %bitcast_clamp_fusion), kind=kCustom, calls=%fused_computation.3 | custom fusion | bytes 24576 | tf_op jit(solution)/shard_map/gather | solution.py:96
  66.8 0.4 iota_compare_fusion
  67.2 12.5 %reduce-precision_convert_fusion = (bf16[2,1024,3,1024]{1,3,2,0:T(8,128)(2,1)}, bf16[2,1024,3,1024]{1,3,2,0:T(8,128)(2,1)}) fusion(f32[2,1024,1024]{1,2,0:T(8,128)} %copy.19, bf16[2,1024,3,128]{3,1,2,0:T(8,128)(2,1)S(1)} %bitcast.121, bf16[1024,128]{1,0:T(8,128)(2,1)S(1)} %gather_fusion.1), kind=kOutput, calls=%fused_computation.5 | convolution fusion | flops 1642070016 | bytes 35389440 | tf_op jit(solution)/shard_map/dot_general | solution.py:72
  79.8 31.5 %fusion.43 = (bf16[3,1024,4,1024]{3,1,0,2:T(8,128)(2,1)}, bf16[3,1024,4,1024,1,1]{3,1,0,2,5,4:T(8,128)(2,1)}, bf16[4,1024,3,1024]{1,3,2,0:T(8,128)(2,1)}) fusion(bf16[2,1024,3,1024]{1,3,2,0:T(8,128)(2,1)} %get-tuple-element.92, bf16[2,1024,3,1024]{1,3,2,0:T(8,128)(2,1)} %get-tuple-element.91), kind=kLoop, calls=%fused_computation.96 | loop fusion | flops 12582912 | bytes 100663296 | tf_op jit(solution)/shard_map/dot_general | solution.py:101
  111.3 13.6 %fusion.10 = f32[384,3072]{1,0:T(8,128)S(1)} fusion(bf16[4,1024,3072]{1,2,0:T(8,128)(2,1)} %bitcast.120, pred[2,384,1024]{2,1,0:T(32,128)(4,1)S(1)} %iota_compare_fusion), kind=kOutput, calls=%fused_computation.18 | convolution fusion | flops 9665249280 | bytes 30670848 | tf_op jit(solution)/shard_map/dot_general | solution.py:101
  124.9 1.8 fusion.46
  126.7 4.8 %squeeze.16 = f32[3,64,3,1024]{3,2,1,0:T(4,128)} reshape(f32[192,3072]{1,0:T(8,128)} %get-tuple-element.97) | data formatting | bytes 4718592 | tf_op jit(solution)/shard_map/squeeze | solution.py:109
  131.5 4.6 %copy.24 = f32[3,64,3,1024]{3,1,2,0:T(8,128)} copy(f32[3,64,3,1024]{3,2,1,0:T(4,128)} %squeeze.16) | data formatting | bytes 4718592 | tf_op jit(solution)/shard_map/squeeze | solution.py:109
  136.1 5.3 %collective-permute-start = (f32[3,64,3,1024]{3,1,2,0:T(8,128)}, f32[3,64,3,1024]{3,1,2,0:T(8,128)}, u32[]{:S(2)}, u32[]{:S(2)}) collective-permute-start(f32[3,64,3,1024]{3,1,2,0:T(8,128)} %copy.24), channel_id=1, source_target_pairs={{0,15},{1,0},{2,1},{3,2},{4,3},{5,4},{6,5},{7,6},{8,7},{9,8},{10,9... | collective-permute-start | bytes 7077896 | tf_op jit(solution)/shard_map/ppermute | solution.py:10
  141.4 3.1 squeeze.17
  144.5 4.7 %copy.25 = f32[3,64,3,1024]{3,1,2,0:T(8,128)} copy(f32[3,64,3,1024]{3,2,1,0:T(4,128)} %squeeze.17) | data formatting | bytes 4718592 | tf_op jit(solution)/shard_map/squeeze | solution.py:110
  149.2 0.3 iota_compare_fusion.1
  149.5 1.3 pad_add_fusion
  150.7 0.1 iota_compare_fusion.2
  151.0 13.1 %fusion.15 = f32[2,2,64,3,1024]{4,2,3,1,0:T(8,128)} fusion(bf16[3,1024,4,1024,1,1]{3,1,0,2,5,4:T(8,128)(2,1)} %get-tuple-element.94, pred[2,2,64,4,1024,1]{4,2,1,0,3,5:T(32,128)(4,1)} %bitcast.125), kind=kOutput, calls=%fused_computation.25 | convolution fusion | flops 6442450944 | bytes 29360128 | tf_op jit(solution)/shard_map/dot_general | solution.py:101
  164.1 4.0 %collective-permute-done = f32[3,64,3,1024]{3,1,2,0:T(8,128)} collective-permute-done((f32[3,64,3,1024]{3,1,2,0:T(8,128)}, f32[3,64,3,1024]{3,1,2,0:T(8,128)}, u32[]{:S(2)}, u32[]{:S(2)}) %collective-permute-start) | collective-permute-done | bytes 2359328 | tf_op jit(solution)/shard_map/ppermute | solution.py:10
  168.1 3.4 fusion.23
  171.5 7.4 %collective-permute-done.1 = f32[3,64,3,1024]{3,1,2,0:T(8,128)S(1)} collective-permute-done((f32[3,64,3,1024]{3,1,2,0:T(8,128)}, f32[3,64,3,1024]{3,1,2,0:T(8,128)S(1)}, u32[]{:S(2)}, u32[]{:S(2)}) %collective-permute-start.1) | collective-permute-done | bytes 2359328 | tf_op jit(solution)/shard_map/ppermute | solution.py:10
  178.9 3.7 fusion.20
  182.5 4.1 %slice_bitcast_fusion.1 = (f32[2,64,3,1024]{3,1,2,0:T(8,128)}, f32[2,64,3,1024]{3,1,2,0:T(8,128)}) fusion(f32[2,2,64,3,1024]{4,2,3,1,0:T(8,128)} %fusion.20), kind=kLoop, calls=%fused_computation.27 | loop fusion | bytes 6291456 | tf_op jit(solution)/shard_map/squeeze | solution.py:118
  186.6 1.5 collective-permute-start.3
  188.1 1.4 collective-permute-start.2
  189.5 14.0 %fusion.3 = f32[2,64,3,1024,1]{3,1,4,2,0:T(8,128)} fusion(bf16[3,1024,4,1024]{3,1,0,2:T(8,128)(2,1)} %get-tuple-element.93, pred[2,64,4,1024,1]{3,1,0,2,4:T(32,128)(4,1)S(1)} %bitcast.127), kind=kOutput, calls=%fused_computation.10 | convolution fusion | flops 3221225472 | bytes 27262976 | tf_op jit(solution)/shard_map/dot_general | solution.py:101
  203.5 1.4 copy.67
  205.2 0.6 compare_reduce_fusion
  205.8 0.6 fusion.39
  206.5 1.5 fusion.28
  207.9 1.3 fusion.26
  209.3 15.8 %collective-permute-done.3 = f32[2,64,3,1024]{3,1,2,0:T(8,128)} collective-permute-done((f32[2,64,3,1024]{3,1,2,0:T(8,128)}, f32[2,64,3,1024]{3,1,2,0:T(8,128)}, u32[]{:S(2)}, u32[]{:S(2)}) %collective-permute-start.3) | collective-permute-done | bytes 1572896 | tf_op jit(solution)/shard_map/ppermute | solution.py:10
  225.1 25.7 %collective-permute-done.2 = f32[2,64,3,1024]{3,1,2,0:T(8,128)} collective-permute-done((f32[2,64,3,1024]{3,1,2,0:T(8,128)}, f32[2,64,3,1024]{3,1,2,0:T(8,128)}, u32[]{:S(2)}, u32[]{:S(2)}) %collective-permute-start.2) | collective-permute-done | bytes 1572896 | tf_op jit(solution)/shard_map/ppermute | solution.py:10
  250.8 3.3 broadcast_multiply_fusion
  254.1 0.7 copy.30
  254.8 15.6 %reshape_reshape.2 = bf16[384,8,16,8]{3,2,1,0:T(8,128)(2,1)} reshape(bf16[1,2,64,3,1024]{4,3,2,1,0:T(4,128)(2,1)S(1)} %copy.30) | data formatting | bytes 1572864 | tf_op jit(solution)/shard_map/reshape;reshape | solution.py:136
  270.3 0.7 reshape.624
  271.0 14.3 %copy.31 = bf16[384,16,8,8]{0,3,2,1:T(8,128)(2,1)S(1)} copy(bf16[384,16,8,8]{3,1,2,0:T(8,128)(2,1)} %bitcast.118) | data formatting | bytes 1572864 | tf_op jit(solution)/shard_map/transpose | solution.py:136
  285.3 0.3 concatenate.39
  285.7 1.4 fusion.48
  287.1 2.1 copy-done.5
  289.3 1.5 slice_select_fusion
  290.7 2.2 scatter.4
  293.0 66.7 %reduce-scatter.2.cloned.1.call-done = f32[64,1152]{1,0:T(8,128)} async-done(((f32[1024,1152]{1,0:T(8,128)}), f32[64,1152]{1,0:T(8,128)}) %reduce-scatter.2.cloned.1.call-update) | async-done | bytes 294928 | tf_op jit(solution)/shard_map/reduce_scatter | solution.py:150
  359.8 1.0 slice_select_fusion.1
  360.8 0.6 collective-permute-start.4
  361.4 6.9 %collective-permute-done.4 = f32[32,1152]{1,0:T(8,128)S(1)} collective-permute-done((f32[32,1152]{1,0:T(8,128)S(1)}, f32[32,1152]{1,0:T(8,128)S(1)}, u32[]{:S(2)}, u32[]{:S(2)}) %collective-permute-start.4) | collective-permute-done | bytes 147488 | tf_op jit(solution)/shard_map/ppermute | solution.py:44
  368.3 1.0 select_add_fusion
  369.3 1.3 collective-permute-start.5
  370.6 3.2 collective-permute-done.5
  373.8 1.5 collective-permute-start.6
  375.3 2.5 collective-permute-done.6
  377.8 0.2 slice_reduce_fusion.1
  378.1 3.0 collective-permute-start.7
  381.1 2.4 collective-permute-done.7
  383.7 0.6 slice.304
  384.3 0.6 slice_reduce_fusion
  (44 shorter events, 1.1 us)
Async XLA Ops:
  7.2 2.5 copy-start
  7.2 352.6 %reduce-scatter.2.cloned.1.call-start = ((), (), s32[]{:S(2)}) async-start(), calls=%async_computation.1 | async-start | bytes 5013504 | tf_op jit(solution)/shard_map/reduce_scatter | solution.py:150
  27.0 1.8 copy-start.3
  28.8 12.7 %copy-start.4 = (s32[12]{0:T(128)S(1)}, s32[12]{0:T(128)}, u32[]{:S(2)}) copy-start(s32[12]{0:T(128)} %constant.302.clone) | copy-start | bytes 148
  41.4 12.7 %copy-start.2 = (s32[12]{0:T(128)S(1)}, s32[12]{0:T(128)}, u32[]{:S(2)}) copy-start(s32[12]{0:T(128)} %constant.301.clone) | copy-start | bytes 148
  136.1 32.0 %collective-permute-start = (f32[3,64,3,1024]{3,1,2,0:T(8,128)}, f32[3,64,3,1024]{3,1,2,0:T(8,128)}, u32[]{:S(2)}, u32[]{:S(2)}) collective-permute-start(f32[3,64,3,1024]{3,1,2,0:T(8,128)} %copy.24), channel_id=1, source_target_pairs={{0,15},{1,0},{2,1},{3,2},{4,3},{5,4},{6,5},{7,6},{8,7},{9,8},{10,9... | collective-permute-start | bytes 7077896 | tf_op jit(solution)/shard_map/ppermute | solution.py:10
  149.2 29.7 %collective-permute-start.1 = (f32[3,64,3,1024]{3,1,2,0:T(8,128)}, f32[3,64,3,1024]{3,1,2,0:T(8,128)S(1)}, u32[]{:S(2)}, u32[]{:S(2)}) collective-permute-start(f32[3,64,3,1024]{3,1,2,0:T(8,128)} %copy.25), channel_id=1, source_target_pairs={{0,1},{1,2},{2,3},{3,4},{4,5},{5,6},{6,7},{7,8},{8,9},{9,10},{10,1... | collective-permute-start | bytes 7077896 | tf_op jit(solution)/shard_map/ppermute | solution.py:10
  178.9 7.7 %copy-start.6 = (f32[3,64,3,1024]{3,1,2,0:T(8,128)}, f32[3,64,3,1024]{3,1,2,0:T(8,128)S(1)}, u32[]{:S(2)}) copy-start(f32[3,64,3,1024]{3,1,2,0:T(8,128)S(1)} %collective-permute-done.1) | copy-start | bytes 7077892
  186.6 38.5 %collective-permute-start.3 = (f32[2,64,3,1024]{3,1,2,0:T(8,128)}, f32[2,64,3,1024]{3,1,2,0:T(8,128)}, u32[]{:S(2)}, u32[]{:S(2)}) collective-permute-start(f32[2,64,3,1024]{3,1,2,0:T(8,128)} %get-tuple-element.99), channel_id=1, source_target_pairs={{0,16},{16,32},{32,48},{48,64},{64,80},{80,96},{96,112},{112,0},{1... | collective-permute-start | bytes 4718600 | tf_op jit(solution)/shard_map/ppermute | solution.py:10
  188.1 62.7 %collective-permute-start.2 = (f32[2,64,3,1024]{3,1,2,0:T(8,128)}, f32[2,64,3,1024]{3,1,2,0:T(8,128)}, u32[]{:S(2)}, u32[]{:S(2)}) collective-permute-start(f32[2,64,3,1024]{3,1,2,0:T(8,128)} %get-tuple-element.98), channel_id=1, source_target_pairs={{0,112},{16,0},{32,16},{48,32},{64,48},{80,64},{96,80},{112,96},{1... | collective-permute-start | bytes 4718600 | tf_op jit(solution)/shard_map/ppermute | solution.py:10
  203.5 1.4 copy-start.7
  203.5 2.3 copy-start.8
  287.1 2.1 copy-start.5
  293.0 91.9 %copy-start.1 = (bf16[2048,128]{1,0:T(8,128)(2,1)S(1)}, bf16[2048,128]{1,0:T(8,128)(2,1)}, u32[]{:S(2)}) copy-start(bf16[2048,128]{1,0:T(8,128)(2,1)} %param.29) | copy-start | bytes 1572868
  360.8 7.5 %collective-permute-start.4 = (f32[32,1152]{1,0:T(8,128)S(1)}, f32[32,1152]{1,0:T(8,128)S(1)}, u32[]{:S(2)}, u32[]{:S(2)}) collective-permute-start(f32[32,1152]{1,0:T(8,128)S(1)} %slice_select_fusion.1), channel_id=1, source_target_pairs={{0,64},{16,80},{32,96},{48,112},{64,0},{80,16},{96,32},{112,48},{1... | collective-permute-start | bytes 442376 | tf_op jit(solution)/shard_map/ppermute | solution.py:44
  369.3 4.4 %collective-permute-start.5 = (f32[16,1152]{1,0:T(8,128)S(1)}, f32[16,1152]{1,0:T(8,128)S(1)}, u32[]{:S(2)}, u32[]{:S(2)}) collective-permute-start(f32[16,1152]{1,0:T(8,128)S(1)} %slice_select_fusion.2), channel_id=1, source_target_pairs={{0,32},{16,48},{32,0},{48,16},{64,96},{80,112},{96,64},{112,80},{1... | collective-permute-start | bytes 221192 | tf_op jit(solution)/shard_map/ppermute | solution.py:44
  373.8 4.0 %collective-permute-start.6 = (f32[8,1152]{1,0:T(8,128)S(1)}, f32[8,1152]{1,0:T(8,128)S(1)}, u32[]{:S(2)}, u32[]{:S(2)}) collective-permute-start(f32[8,1152]{1,0:T(8,128)S(1)} %slice_select_fusion.3), channel_id=1, source_target_pairs={{0,16},{16,0},{32,48},{48,32},{64,80},{80,64},{96,112},{112,96},{1... | collective-permute-start | bytes 110600 | tf_op jit(solution)/shard_map/ppermute | solution.py:44
  378.1 5.5 %collective-permute-start.7 = (f32[8,1152]{1,0:T(8,128)S(1)}, f32[8,1152]{1,0:T(8,128)S(1)}, u32[]{:S(2)}, u32[]{:S(2)}) collective-permute-start(f32[8,1152]{1,0:T(8,128)S(1)} %broadcast_divide_fusion), channel_id=1, source_target_pairs={{0,128},{128,0},{1,129},{129,1},{2,130},{130,2},{3,131},{131,3},{4... | collective-permute-start | bytes 110600 | tf_op jit(solution)/shard_map/ppermute | solution.py:51
Sparse Core Ops, SparseCore 0:
  293.1 66.5 reduce-scatter.1

commit v3 on v1

--- a/solution.py
+++ b/solution.py
@@ -64,19 +64,7 @@
     flat_valid = valid.reshape(tile_count, 64)
     flat_desc = descriptors.reshape(tile_count, 64, desc_width)
     flat_desc = jnp.where(flat_valid[:, :, None] != 0, flat_desc, jnp.zeros_like(flat_desc))
-    scores = lax.dot_general(
-        flat_desc, sparse, (((2,), (1,)), ((), ())), preferred_element_type=jnp.float32
-    )
     flat_deriv = derivatives.reshape(tile_count, rows, 3, desc_width)
-    projected = lax.dot_general(
-        flat_deriv, sparse, (((3,), (1,)), ((), ())), preferred_element_type=jnp.float32
-    )
-    scores_rep = jnp.repeat(scores, slot_total, axis=1)
-    contribution = (-2.0 * scores_rep)[:, :, None, :] * projected
-    high_wide = lax.reduce_precision(contribution, exponent_bits=8, mantissa_bits=7)
-    high = high_wide.astype(jnp.bfloat16)
-    low = (contribution - high_wide).astype(jnp.bfloat16)
-    parts = jnp.concatenate([high, low], axis=0).reshape(2 * tile_count, rows, 3 * sparse_count)
 
     tile_ids = jnp.arange(tile_count, dtype=jnp.int32)
     tile_x = (tile_ids // tiles_y)[:, None]
@@ -91,11 +79,33 @@
         jnp.arange(ext_rows, dtype=jnp.int32)[None, :, None] == target[:, None, :]
     ).astype(jnp.bfloat16)
     onehot = jnp.concatenate([onehot, onehot], axis=0)
-    accumulator = lax.dot_general(
-        onehot, parts, (((0, 2), (0, 1)), ((), ())), preferred_element_type=jnp.float32
+
+    def owned_part(sparse_part):
+        width = sparse_part.shape[0]
+        scores = lax.dot_general(
+            flat_desc, sparse_part, (((2,), (1,)), ((), ())), preferred_element_type=jnp.float32
+        )
+        projected = lax.dot_general(
+            flat_deriv, sparse_part, (((3,), (1,)), ((), ())), preferred_element_type=jnp.float32
+        )
+        scores_rep = jnp.repeat(scores, slot_total, axis=1)
+        contribution = (-2.0 * scores_rep)[:, :, None, :] * projected
+        high_wide = lax.reduce_precision(contribution, exponent_bits=8, mantissa_bits=7)
+        high = high_wide.astype(jnp.bfloat16)
+        low = (contribution - high_wide).astype(jnp.bfloat16)
+        parts = jnp.concatenate([high, low], axis=0).reshape(2 * tile_count, rows, 3 * width)
+        accumulator = lax.dot_general(
+            onehot, parts, (((0, 2), (0, 1)), ((), ())), preferred_element_type=jnp.float32
+        )
+        extended = accumulator.reshape(tiles_x + 2, tiles_y + 2, 64, 3, width)
+        return fold_x(fold_y(extended))
+
+    chunks = 2
+    chunk_width = sparse_count // chunks
+    owned = jnp.concatenate(
+        [owned_part(sparse[c * chunk_width : (c + 1) * chunk_width]) for c in range(chunks)],
+        axis=-1,
     )
-    extended = accumulator.reshape(tiles_x + 2, tiles_y + 2, 64, 3, sparse_count)
-    owned = fold_x(fold_y(extended))
     design = owned.astype(jnp.bfloat16)
 
     valid_own = valid[0]

time: 302 us -> 288 us (0.954)
  waiting for transfers between devices: 167 us -> 133 us
  matrix products: 42.7 us -> 49.4 us
  starting transfers between devices: 13.7 us -> 18.8 us
  other arithmetic: 19.7 us -> 23.5 us
  local copies, waits for them, and re-layouts: 43 us -> 46.4 us
    ppermute x4 -> x8, waiting for transfers between devices: 85.2 us -> 54.4 us  [passed_along(): lax.ppermute(x, axis, [(i, (i + by) % length) for i in range(length)])]
    dot_general x3 -> x6, matrix products: 39.1 us -> 44.7 us  [the longest x2 30.5 us: owned_part(): lax.dot_general(onehot, parts, (((0, 2), (0, 1)), ((), ())), preferred_el...]
    ppermute x4 -> x8, starting transfers between devices: 7.35 us -> 12.3 us  [passed_along(): lax.ppermute(x, axis, [(i, (i + by) % length) for i in range(length)])]
    another operation x3 -> x5, other arithmetic: 1.93 us -> 5.53 us
    mul x1 -> x0, other arithmetic: 3.31 us -> none  [per_device(): masked = design * valid_own[:, :, :, None, None].astype(jnp.bfloat16)]
    mul x1 -> x2, local copies, waits for them, and re-layouts: 8.69 us -> 10.8 us  [owned_part(): contribution = (-2.0 * scores_rep)[:, :, None, :] * projected]
  transfers between devices with their start and end apart: 9 -> 13, of which waited for: 9 -> 11; matrix products, arithmetic and copies ran while one was open for 1% -> 16% of each run, Pallas kernels for 0% -> 0%
where the time goes in v3:
time: 288 us; the launch traced here: 287 us
  waiting for transfers between devices  133 us (46%)
  matrix products  49.4 us (17%)
  local copies, waits for them, and re-layouts  46.4 us (16%)
  other arithmetic  23.5 us (8%)
  starting transfers between devices  18.8 us (7%)
  between operations  15.7 us (5%)
    reduce_scatter x1, waiting for transfers between devices, per_device(): reduced = lax.psum_scatter(packed, 'gy', scatter_dimension=0, tiled=True)  64.8 us
    ppermute x8, waiting for transfers between devices, passed_along(): lax.ppermute(x, axis, [(i, (i + by) % length) for i in range(length)])  54.4 us
    dot_general x2, matrix products, owned_part(): lax.dot_general(onehot, parts, (((0, 2), (0, 1)), ((), ())), preferred_el...  30.5 us
    dot_general x2, matrix products, owned_part(): lax.dot_general(flat_deriv, sparse_part, (((3,), (1,)), ((), ())), prefer...  13 us
    ppermute x3, waiting for transfers between devices, halving_scatter(): block = keep + lax.ppermute(send, axis, pairs)  12.6 us
    ppermute x8, starting transfers between devices, passed_along(): lax.ppermute(x, axis, [(i, (i + by) % length) for i in range(length)])  12.3 us
    mul x2, local copies, waits for them, and re-layouts, owned_part(): contribution = (-2.0 * scores_rep)[:, :, None, :] * projected  10.8 us
    concatenate x1, local copies, waits for them, and re-layouts, per_device(): packed = jnp.concatenate([gram_part, extra], axis=1)  6.17 us
  transfers between devices with their start and end apart: 13, of which 11 were waited for; matrix products, arithmetic and copies ran while one was open for 16% of the time, Pallas kernels for 0%

profile of v3, /device:TPU:16, one launch (start us, length us, event | category | flops | bytes accessed | tf_op | source)
XLA Modules:
  0.0 287.0 jit_solution(9880181522393678162)
XLA Ops:
  7.2 0.7 fusion.50
  8.0 0.7 compare_bitcast_fusion
  8.7 3.2 %gather_fusion = bf16[1024,128]{1,0:T(8,128)(2,1)S(1)} fusion(bf16[2048,128]{1,0:T(8,128)(2,1)S(1)} %copy-done, s32[1024]{0:T(1024)S(1)} %fusion.50), kind=kCustom, calls=%fused_computation | custom fusion | bytes 528384 | tf_op jit(solution)/shard_map/gather | solution.py:59
  11.9 1.0 convolution_multiply_fusion.1
  12.9 2.5 broadcast_in_dim.32
  15.4 5.4 %copy.60 = f32[2,1024,512]{1,2,0:T(8,128)} copy(f32[2,1024,512]{2,1,0:T(8,128)} %bitcast.157) | data formatting | bytes 8388608 | tf_op jit(solution)/shard_map/mul | solution.py:92
  20.8 1.7 copy.61
  22.8 0.9 iota_compare_fusion
  23.7 2.7 pad_add_fusion
  26.4 5.7 %reduce-precision_convert_fusion.1 = (bf16[2,1024,3,512]{1,3,2,0:T(8,128)(2,1)}, bf16[2,1024,3,512]{1,3,2,0:T(8,128)(2,1)}) fusion(f32[2,1024,512]{1,2,0:T(8,128)S(1)} %copy-done.2, bf16[2,1024,3,128]{3,1,2,0:T(8,128)(2,1)S(1)} %bitcast.161, bf16[1024,128]{1,0:T(8,128)(2,1)S(1)} %gather_fusion), kind=kOutput, calls=%fused_computation.4 | convolution fusion | flops 821035008 | bytes 18481152 | tf_op jit(solution)/shard_map/dot_general | solution.py:88
  32.1 15.2 %fusion.8 = f32[3,4,64,3,512]{4,2,3,1,0:T(8,128)} fusion(pred[3,4,64,4,1024,1]{4,2,1,0,3,5:T(32,128)(4,1)} %bitcast.167, bf16[2,1024,3,512]{1,3,2,0:T(8,128)(2,1)} %get-tuple-element.124, bf16[2,1024,3,512]{1,3,2,0:T(8,128)(2,1)} %get-tuple-element.123), kind=kOutput, calls=%fused_computation.20 | convolution fusion | flops 9669967872 | bytes 20447232 | tf_op jit(solution)/shard_map/dot_general | solution.py:97
  47.3 3.3 %slice_bitcast_fusion.2 = (f32[3,64,3,512]{3,1,2,0:T(8,128)}, f32[3,64,3,512]{3,1,2,0:T(8,128)}) fusion(f32[3,4,64,3,512]{4,2,3,1,0:T(8,128)} %fusion.8), kind=kLoop, calls=%fused_computation.29 | loop fusion | bytes 4718592 | tf_op jit(solution)/shard_map/squeeze | solution.py:25
  50.7 5.3 %collective-permute-start = (f32[3,64,3,512]{3,1,2,0:T(8,128)}, f32[3,64,3,512]{3,1,2,0:T(8,128)S(1)}, u32[]{:S(2)}, u32[]{:S(2)}) collective-permute-start(f32[3,64,3,512]{3,1,2,0:T(8,128)} %get-tuple-element.128), channel_id=1, source_target_pairs={{0,15},{1,0},{2,1},{3,2},{4,3},{5,4},{6,5},{7,6},{8,7},{9,8},{10,9... | collective-permute-start | bytes 3538952 | tf_op jit(solution)/shard_map/ppermute | solution.py:9
  56.2 2.5 broadcast_in_dim.33
  58.7 5.4 %copy.69 = f32[2,1024,512]{1,2,0:T(8,128)} copy(f32[2,1024,512]{2,1,0:T(8,128)} %bitcast.158) | data formatting | bytes 8388608 | tf_op jit(solution)/shard_map/mul | solution.py:92
  64.1 7.3 %reduce-precision_convert_fusion = (bf16[2,1024,3,512]{1,3,2,0:T(8,128)(2,1)}, bf16[2,1024,3,512]{1,3,2,0:T(8,128)(2,1)}) fusion(f32[2,1024,512]{1,2,0:T(8,128)} %copy.69, bf16[2,1024,3,128]{3,1,2,0:T(8,128)(2,1)S(1)} %bitcast.162, bf16[1024,128]{1,0:T(8,128)(2,1)S(1)} %gather_fusion), kind=kOutput, calls=%fused_computation.2 | convolution fusion | flops 821035008 | bytes 18481152 | tf_op jit(solution)/shard_map/dot_general | solution.py:88
  71.4 15.3 %fusion.13 = f32[3,4,64,3,512]{4,2,3,1,0:T(8,128)} fusion(pred[3,4,64,4,1024,1]{4,2,1,0,3,5:T(32,128)(4,1)} %bitcast.168, bf16[2,1024,3,512]{1,3,2,0:T(8,128)(2,1)} %get-tuple-element.126, bf16[2,1024,3,512]{1,3,2,0:T(8,128)(2,1)} %get-tuple-element.125), kind=kOutput, calls=%fused_computation.21 | convolution fusion | flops 9669967872 | bytes 20447232 | tf_op jit(solution)/shard_map/dot_general | solution.py:97
  86.7 1.8 slice_bitcast_fusion
  88.6 3.0 %collective-permute-start.4 = (f32[3,64,3,512]{3,1,2,0:T(8,128)S(1)}, f32[3,64,3,512]{3,1,2,0:T(8,128)S(1)}, u32[]{:S(2)}, u32[]{:S(2)}) collective-permute-start(f32[3,64,3,512]{3,1,2,0:T(8,128)S(1)} %get-tuple-element.130), channel_id=1, source_target_pairs={{0,15},{1,0},{2,1},{3,2},{4,3},{5,4},{6,5},{7,6},{8,7},{9,8},{10,9... | collective-permute-start | bytes 3538952 | tf_op jit(solution)/shard_map/ppermute | solution.py:9
  91.5 1.7 slice-done.3
  93.5 1.7 fusion.22
  95.2 1.7 fusion.20
  97.0 1.5 slice_bitcast_fusion.8
  98.5 1.4 collective-permute-start.2
  99.8 0.6 collective-permute-start.3
  100.5 4.8 %collective-permute-done.4 = f32[3,64,3,512]{3,1,2,0:T(8,128)S(1)} collective-permute-done((f32[3,64,3,512]{3,1,2,0:T(8,128)S(1)}, f32[3,64,3,512]{3,1,2,0:T(8,128)S(1)}, u32[]{:S(2)}, u32[]{:S(2)}) %collective-permute-start.4) | collective-permute-done | bytes 1179680 | tf_op jit(solution)/shard_map/ppermute | solution.py:9
  105.5 2.8 collective-permute-done.5
  108.4 0.3 fusion.18
  108.7 1.4 slice_bitcast_fusion.6
  110.0 1.4 collective-permute-start.6
  111.4 0.6 collective-permute-start.7
  112.7 0.9 compare_reduce_fusion
  113.6 0.6 fusion.51
  115.5 0.6 compare_reduce_fusion.1
  116.1 3.0 %collective-permute-done.2 = f32[2,64,3,512]{3,1,2,0:T(8,128)} collective-permute-done((f32[2,64,3,512]{3,1,2,0:T(8,128)}, f32[2,64,3,512]{3,1,2,0:T(8,128)}, u32[]{:S(2)}, u32[]{:S(2)}) %collective-permute-start.2) | collective-permute-done | bytes 786464 | tf_op jit(solution)/shard_map/ppermute | solution.py:9
  119.2 16.7 %collective-permute-done.3 = f32[2,64,3,512]{3,1,2,0:T(8,128)} collective-permute-done((f32[2,64,3,512]{3,1,2,0:T(8,128)}, f32[2,64,3,512]{3,1,2,0:T(8,128)}, u32[]{:S(2)}, u32[]{:S(2)}) %collective-permute-start.3) | collective-permute-done | bytes 786464 | tf_op jit(solution)/shard_map/ppermute | solution.py:9
  135.9 1.8 fusion.27
  137.7 0.3 copy.74
  138.1 1.1 concatenate.78
  139.2 13.7 %collective-permute-done.6 = f32[2,64,3,512]{3,1,2,0:T(8,128)} collective-permute-done((f32[2,64,3,512]{3,1,2,0:T(8,128)}, f32[2,64,3,512]{3,1,2,0:T(8,128)}, u32[]{:S(2)}, u32[]{:S(2)}) %collective-permute-start.6) | collective-permute-done | bytes 786464 | tf_op jit(solution)/shard_map/ppermute | solution.py:9
  152.9 13.3 %collective-permute-done.7 = f32[2,64,3,512]{3,1,2,0:T(8,128)} collective-permute-done((f32[2,64,3,512]{3,1,2,0:T(8,128)}, f32[2,64,3,512]{3,1,2,0:T(8,128)}, u32[]{:S(2)}, u32[]{:S(2)}) %collective-permute-start.7) | collective-permute-done | bytes 786464 | tf_op jit(solution)/shard_map/ppermute | solution.py:9
  166.2 1.6 fusion.24
  167.8 0.3 copy.75
  168.1 0.3 concatenate.79
  168.5 1.3 fusion.30
  169.8 0.7 broadcast_select_fusion
  170.5 3.4 %convolution_bitcast_fusion = f32[1024,1024]{0,1:T(8,128)} fusion(bf16[2,64,3,512]{3,1,2,0:T(8,128)(2,1)S(1)} %bitcast.165, bf16[2,64,3,512]{3,1,2,0:T(8,128)(2,1)S(1)} %bitcast.163, bf16[2,64]{1,0:T(2,128)(2,1)S(1)} %get-tuple-element.136), kind=kOutput, calls=%fused_computation.22 | convolution fusion | flops 807665664 | bytes 4980992 | tf_op jit(solution)/shard_map/dot_general | solution.py:116
  174.0 5.0 %pad_maximum_fusion = f32[1024,1152]{0,1:T(8,128)} fusion(f32[1024,128]{0,1:T(8,128)S(1)} %scatter.9, f32[1024,1024]{0,1:T(8,128)} %convolution_bitcast_fusion), kind=kLoop, calls=%fused_computation.19 | loop fusion | flops 1179648 | bytes 9437184 | tf_op jit(solution)/shard_map/concatenate | solution.py:124
  179.1 6.2 %copy.77 = f32[1024,1152]{1,0:T(8,128)} copy(f32[1024,1152]{0,1:T(8,128)} %pad_maximum_fusion) | data formatting | bytes 9437184 | tf_op jit(solution)/shard_map/concatenate | solution.py:124
  185.2 4.9 %copy.78 = f32[16,8,8,1152]{3,2,1,0:T(8,128)} copy(f32[16,8,8,1152]{3,2,0,1:T(8,128)} %bitcast.156) | data formatting | bytes 9437184 | tf_op jit(solution)/shard_map/transpose | solution.py:127
  190.2 64.8 %reduce-scatter.2.cloned.1.call-done = f32[64,1152]{1,0:T(8,128)} async-done(((f32[1024,1152]{1,0:T(8,128)}), f32[64,1152]{1,0:T(8,128)}) %reduce-scatter.2.cloned.1.call-update) | async-done | bytes 294928 | tf_op jit(solution)/shard_map/reduce_scatter | solution.py:129
  255.0 1.0 slice_select_fusion
  256.0 0.6 collective-permute-start.8
  256.6 6.9 %collective-permute-done.8 = f32[32,1152]{1,0:T(8,128)S(1)} collective-permute-done((f32[32,1152]{1,0:T(8,128)S(1)}, f32[32,1152]{1,0:T(8,128)S(1)}, u32[]{:S(2)}, u32[]{:S(2)}) %collective-permute-start.8) | collective-permute-done | bytes 147488 | tf_op jit(solution)/shard_map/ppermute | solution.py:43
  263.6 1.0 select_add_fusion
  264.6 1.3 collective-permute-start.9
  265.8 3.2 %collective-permute-done.9 = f32[16,1152]{1,0:T(8,128)S(1)} collective-permute-done((f32[16,1152]{1,0:T(8,128)S(1)}, f32[16,1152]{1,0:T(8,128)S(1)}, u32[]{:S(2)}, u32[]{:S(2)}) %collective-permute-start.9) | collective-permute-done | bytes 73760 | tf_op jit(solution)/shard_map/ppermute | solution.py:43
  269.1 1.6 collective-permute-start.10
  270.6 2.5 collective-permute-done.10
  273.4 3.0 %collective-permute-start.11 = (f32[8,1152]{1,0:T(8,128)S(1)}, f32[8,1152]{1,0:T(8,128)S(1)}, u32[]{:S(2)}, u32[]{:S(2)}) collective-permute-start(f32[8,1152]{1,0:T(8,128)S(1)} %broadcast_divide_fusion), channel_id=1, source_target_pairs={{0,128},{128,0},{1,129},{129,1},{2,130},{130,2},{3,131},{131,3},{4... | collective-permute-start | bytes 110600 | tf_op jit(solution)/shard_map/ppermute | solution.py:50
  276.4 1.0 pad_maximum_fusion.1
  277.4 1.5 collective-permute-done.11
  278.9 0.6 slice.398
  279.6 0.6 slice_reduce_fusion
  (56 shorter events, 2.3 us)
Async XLA Ops:
  7.2 1.5 copy-start
  7.2 247.8 %reduce-scatter.2.cloned.1.call-start = ((), (), s32[]{:S(2)}) async-start(), calls=%async_computation.1 | async-start | bytes 5013504 | tf_op jit(solution)/shard_map/reduce_scatter | solution.py:129
  20.8 1.7 copy-start.7
  22.8 3.6 %copy-start.2 = (f32[2,1024,512]{1,2,0:T(8,128)S(1)}, f32[2,1024,512]{1,2,0:T(8,128)}, u32[]{:S(2)}) copy-start(f32[2,1024,512]{1,2,0:T(8,128)} %copy.60) | copy-start | bytes 12582916
  47.3 8.6 %copy-start.6 = (bf16[1,1,2,64,128]{4,3,2,1,0:T(8,128)(2,1)S(1)}, bf16[1,1,2,64,128]{4,3,2,1,0:T(8,128)(2,1)}, u32[]{:S(2)}) copy-start(bf16[1,1,2,64,128]{4,3,2,1,0:T(8,128)(2,1)} %param.27) | copy-start | bytes 98308
  50.7 42.8 %collective-permute-start = (f32[3,64,3,512]{3,1,2,0:T(8,128)}, f32[3,64,3,512]{3,1,2,0:T(8,128)S(1)}, u32[]{:S(2)}, u32[]{:S(2)}) collective-permute-start(f32[3,64,3,512]{3,1,2,0:T(8,128)} %get-tuple-element.128), channel_id=1, source_target_pairs={{0,15},{1,0},{2,1},{3,2},{4,3},{5,4},{6,5},{7,6},{8,7},{9,8},{10,9... | collective-permute-start | bytes 3538952 | tf_op jit(solution)/shard_map/ppermute | solution.py:9
  56.0 39.2 %collective-permute-start.1 = (f32[3,64,3,512]{3,1,2,0:T(8,128)}, f32[3,64,3,512]{3,1,2,0:T(8,128)}, u32[]{:S(2)}, u32[]{:S(2)}) collective-permute-start(f32[3,64,3,512]{3,1,2,0:T(8,128)} %get-tuple-element.127), channel_id=1, source_target_pairs={{0,1},{1,2},{2,3},{3,4},{4,5},{5,6},{6,7},{7,8},{8,9},{9,10},{10,1... | collective-permute-start | bytes 3538952 | tf_op jit(solution)/shard_map/ppermute | solution.py:9
  88.6 16.7 %collective-permute-start.4 = (f32[3,64,3,512]{3,1,2,0:T(8,128)S(1)}, f32[3,64,3,512]{3,1,2,0:T(8,128)S(1)}, u32[]{:S(2)}, u32[]{:S(2)}) collective-permute-start(f32[3,64,3,512]{3,1,2,0:T(8,128)S(1)} %get-tuple-element.130), channel_id=1, source_target_pairs={{0,15},{1,0},{2,1},{3,2},{4,3},{5,4},{6,5},{7,6},{8,7},{9,8},{10,9... | collective-permute-start | bytes 3538952 | tf_op jit(solution)/shard_map/ppermute | solution.py:9
  91.5 16.8 %collective-permute-start.5 = (f32[3,64,3,512]{3,1,2,0:T(8,128)S(1)}, f32[3,64,3,512]{3,1,2,0:T(8,128)S(1)}, u32[]{:S(2)}, u32[]{:S(2)}) collective-permute-start(f32[3,64,3,512]{3,1,2,0:T(8,128)S(1)} %get-tuple-element.129), channel_id=1, source_target_pairs={{0,1},{1,2},{2,3},{3,4},{4,5},{5,6},{6,7},{7,8},{8,9},{9,10},{10,1... | collective-permute-start | bytes 3538952 | tf_op jit(solution)/shard_map/ppermute | solution.py:9
  91.5 1.7 slice-start.3
  93.2 12.1 %slice-start = ((s8[4718592]{0:T(1024)(128)(4,1)}), s8[524288]{0:T(1024)(128)(4,1)S(1)}, s32[]{:S(2)}) async-start(s8[4718592]{0:T(1024)(128)(4,1)} %bitcast.159), calls=%async_computation.2 | async-start | bytes 1048576
  93.5 11.8 %slice-start.1 = ((s8[4718592]{0:T(1024)(128)(4,1)}), s8[4194304]{0:T(1024)(128)(4,1)S(1)}, s32[]{:S(2)}) async-start(s8[4718592]{0:T(1024)(128)(4,1)} %bitcast.159), calls=%async_computation.3 | async-start | bytes 8388608
  95.2 10.1 %slice-start.2 = ((f32[3,4,64,3,512]{4,2,3,1,0:T(8,128)}), f32[3,2,64,3,512]{4,2,3,1,0:T(8,128)S(1)}, s32[]{:S(2)}) async-start(f32[3,4,64,3,512]{4,2,3,1,0:T(8,128)} %fusion.13), calls=%async_computation.4 | async-start | bytes 4718592 | tf_op jit(solution)/shard_map/slice | solution.py:26
  96.9 8.6 %copy-start.3 = (f32[3,2,64,3,512]{4,2,3,0,1:T(8,128)}, f32[3,2,64,3,512]{4,2,3,0,1:T(8,128)S(1)}, u32[]{:S(2)}) copy-start(f32[3,2,64,3,512]{4,2,3,0,1:T(8,128)S(1)} %fusion.20) | copy-start | bytes 7077892
  98.5 20.7 %collective-permute-start.2 = (f32[2,64,3,512]{3,1,2,0:T(8,128)}, f32[2,64,3,512]{3,1,2,0:T(8,128)}, u32[]{:S(2)}, u32[]{:S(2)}) collective-permute-start(f32[2,64,3,512]{3,1,2,0:T(8,128)} %get-tuple-element.131), channel_id=1, source_target_pairs={{0,112},{16,0},{32,16},{48,32},{64,48},{80,64},{96,80},{112,96},{1... | collective-permute-start | bytes 2359304 | tf_op jit(solution)/shard_map/ppermute | solution.py:9
  99.8 36.1 %collective-permute-start.3 = (f32[2,64,3,512]{3,1,2,0:T(8,128)}, f32[2,64,3,512]{3,1,2,0:T(8,128)}, u32[]{:S(2)}, u32[]{:S(2)}) collective-permute-start(f32[2,64,3,512]{3,1,2,0:T(8,128)} %get-tuple-element.132), channel_id=1, source_target_pairs={{0,16},{16,32},{32,48},{48,64},{64,80},{80,96},{96,112},{112,0},{1... | collective-permute-start | bytes 2359304 | tf_op jit(solution)/shard_map/ppermute | solution.py:9
  105.5 6.6 %copy-start.9 = (s32[1,1,2,64]{3,2,1,0:T(2,128)S(1)}, s32[1,1,2,64]{3,2,1,0:T(2,128)}, u32[]{:S(2)}) copy-start(s32[1,1,2,64]{3,2,1,0:T(2,128)} %param.30) | copy-start | bytes 1540
  105.5 6.9 %copy-start.8 = (bf16[1,1,2,64,3]{3,2,4,1,0:T(2,128)(2,1)S(1)}, bf16[1,1,2,64,3]{3,2,4,1,0:T(2,128)(2,1)}, u32[]{:S(2)}) copy-start(bf16[1,1,2,64,3]{3,2,4,1,0:T(2,128)(2,1)} %param.31) | copy-start | bytes 2308
  110.0 42.8 %collective-permute-start.6 = (f32[2,64,3,512]{3,1,2,0:T(8,128)}, f32[2,64,3,512]{3,1,2,0:T(8,128)}, u32[]{:S(2)}, u32[]{:S(2)}) collective-permute-start(f32[2,64,3,512]{3,1,2,0:T(8,128)} %get-tuple-element.133), channel_id=1, source_target_pairs={{0,112},{16,0},{32,16},{48,32},{64,48},{80,64},{96,80},{112,96},{1... | collective-permute-start | bytes 2359304 | tf_op jit(solution)/shard_map/ppermute | solution.py:9
  111.4 54.8 %collective-permute-start.7 = (f32[2,64,3,512]{3,1,2,0:T(8,128)}, f32[2,64,3,512]{3,1,2,0:T(8,128)}, u32[]{:S(2)}, u32[]{:S(2)}) collective-permute-start(f32[2,64,3,512]{3,1,2,0:T(8,128)} %get-tuple-element.134), channel_id=1, source_target_pairs={{0,16},{16,32},{32,48},{48,64},{64,80},{80,96},{96,112},{112,0},{1... | collective-permute-start | bytes 2359304 | tf_op jit(solution)/shard_map/ppermute | solution.py:9
  167.8 6.1 %copy-start.4 = (bf16[1,2,64,3,512]{4,2,3,1,0:T(8,128)(2,1)}, bf16[1,2,64,3,512]{4,2,3,1,0:T(8,128)(2,1)S(1)}, u32[]{:S(2)}) copy-start(bf16[1,2,64,3,512]{4,2,3,1,0:T(8,128)(2,1)S(1)} %fusion.24) | copy-start | bytes 1179652
  190.2 90.0 %copy-start.1 = (bf16[2048,128]{1,0:T(8,128)(2,1)S(1)}, bf16[2048,128]{1,0:T(8,128)(2,1)}, u32[]{:S(2)}) copy-start(bf16[2048,128]{1,0:T(8,128)(2,1)} %param.32) | copy-start | bytes 1572868
  190.2 86.2 %copy-start.5 = (bf16[1,2,64,3,512]{4,2,3,1,0:T(8,128)(2,1)S(1)}, bf16[1,2,64,3,512]{4,2,3,1,0:T(8,128)(2,1)}, u32[]{:S(2)}) copy-start(bf16[1,2,64,3,512]{4,2,3,1,0:T(8,128)(2,1)} %copy-done.4) | copy-start | bytes 1179652
  256.0 7.5 %collective-permute-start.8 = (f32[32,1152]{1,0:T(8,128)S(1)}, f32[32,1152]{1,0:T(8,128)S(1)}, u32[]{:S(2)}, u32[]{:S(2)}) collective-permute-start(f32[32,1152]{1,0:T(8,128)S(1)} %slice_select_fusion), channel_id=1, source_target_pairs={{0,64},{16,80},{32,96},{48,112},{64,0},{80,16},{96,32},{112,48},{1... | collective-permute-start | bytes 442376 | tf_op jit(solution)/shard_map/ppermute | solution.py:43
  264.6 4.4 %collective-permute-start.9 = (f32[16,1152]{1,0:T(8,128)S(1)}, f32[16,1152]{1,0:T(8,128)S(1)}, u32[]{:S(2)}, u32[]{:S(2)}) collective-permute-start(f32[16,1152]{1,0:T(8,128)S(1)} %slice_select_fusion.1), channel_id=1, source_target_pairs={{0,32},{16,48},{32,0},{48,16},{64,96},{80,112},{96,64},{112,80},{1... | collective-permute-start | bytes 221192 | tf_op jit(solution)/shard_map/ppermute | solution.py:43
  269.1 4.0 %collective-permute-start.10 = (f32[8,1152]{1,0:T(8,128)S(1)}, f32[8,1152]{1,0:T(8,128)S(1)}, u32[]{:S(2)}, u32[]{:S(2)}) collective-permute-start(f32[8,1152]{1,0:T(8,128)S(1)} %slice_select_fusion.2), channel_id=1, source_target_pairs={{0,16},{16,0},{32,48},{48,32},{64,80},{80,64},{96,112},{112,96},{1... | collective-permute-start | bytes 110600 | tf_op jit(solution)/shard_map/ppermute | solution.py:43
  273.4 5.5 %collective-permute-start.11 = (f32[8,1152]{1,0:T(8,128)S(1)}, f32[8,1152]{1,0:T(8,128)S(1)}, u32[]{:S(2)}, u32[]{:S(2)}) collective-permute-start(f32[8,1152]{1,0:T(8,128)S(1)} %broadcast_divide_fusion), channel_id=1, source_target_pairs={{0,128},{128,0},{1,129},{129,1},{2,130},{130,2},{3,131},{131,3},{4... | collective-permute-start | bytes 110600 | tf_op jit(solution)/shard_map/ppermute | solution.py:50
Sparse Core Ops, SparseCore 0:
  190.3 64.6 reduce-scatter.1
